TPU v7x, 128 devices: a whole 4x4x4 slice. The times are simulated.
128 devices in a mesh: term: 4 (over x_hi, core), sec: 32 (over x_lo, z, y).
Axes of the slice: x: 4 (x_hi: 2, x_lo: 2; x = x_hi * 2 + x_lo), y: 4, z: 4, core: 2. Of those that a mesh axis runs over, the one named last changes fastest.
Arguments:
- psi_tiles: bfloat16 [768, 512, 512], P('sec'), may hold values from -6 to 6
- sectors: int32 [768, 2], P('sec'), may hold values from 0 to 15
- sources: int32 [4, 768], P('term', 'sec'), may hold values from 0 to 767, as said below
- left_env: bfloat16 [4, 16, 512, 512], P('term', None, 'sec'), may hold values from -0.25 to 0.25
- right_env: bfloat16 [4, 16, 512, 512], P('term', None, 'sec'), may hold values from -0.25 to 0.25
Outputs:
- applied: bfloat16 [768, 512, 512], P('sec', 'term')
Inputs may be any that keep to these rules, and one draw needn't show every extreme that they name: sources[t, k] lies in the same aligned block of 24 tiles as k, and each row maps each such block one to one onto itself.
All inputs are finite; a program needn't handle non-finite values.
Results may differ from a plain program's by a relative error of at most 0.013.
Values may be sent and summed in bfloat16 or wider, within the bound.
No kernel may reach another device: no remote copies, remote signals or barrier semaphores. Data moves between devices by JAX's collectives and lax.ppermute only.
A program may use at most 192 MiB of HBM per device.

v0:
```python
import jax
import jax.numpy as jnp
from jax import lax
from jax.sharding import PartitionSpec as P


def body(psi_tiles, sectors, sources, left_env, right_env):
    tile_count = psi_tiles.shape[0]
    width = psi_tiles.shape[2]
    local_ids = sources[0] - lax.axis_index("sec") * tile_count
    moved = jnp.take(psi_tiles, local_ids, axis=0)
    left_ids = sectors[:, 0]
    right_ids = sectors[:, 1]
    chosen = jnp.take(lax.all_gather(right_env[0], "sec", axis=1, tiled=True), right_ids, axis=0)
    half = jnp.einsum("kij,kjl->kil", moved, chosen, preferred_element_type=jnp.float32).astype(
        jnp.bfloat16
    )
    chosen = jnp.take(lax.all_gather(left_env[0], "sec", axis=1, tiled=True), left_ids, axis=0)
    term_out = jnp.einsum("kij,kjl->kil", chosen, half, preferred_element_type=jnp.float32)
    share_rows = width // lax.axis_size("term")
    summed = lax.psum(term_out.astype(jnp.bfloat16), "term").astype(jnp.float32)
    kept = lax.dynamic_slice_in_dim(summed, lax.axis_index("term") * share_rows, share_rows, 1)
    return kept.astype(jnp.bfloat16)


def solution(mesh):
    placed = (
        P("sec", None, None),
        P("sec", None),
        P("term", "sec"),
        P("term", None, "sec", None),
        P("term", None, "sec", None),
    )
    return jax.shard_map(
        body, mesh=mesh, in_specs=placed, out_specs=P("sec", "term", None), check_vma=False
    )
```

profile of v0, /device:TPU:1, one launch (start us, length us, event | category | flops | bytes accessed | tf_op | source)
XLA Modules:
  0.0 617.3 jit_solution(6412177317776371115)
XLA Ops:
  6.5 0.0 all-gather.7.cloned.1.call-start
  6.5 0.7 all-gather.7.cloned.1.call-update
  7.3 0.0 all-gather.5.cloned.1.call-start
  7.3 0.7 all-gather.5.cloned.1.call-update
  8.0 0.0 all-reduce.2.cloned.1.call-start
  8.1 0.7 fusion.30
  8.7 0.0 copy-start
  8.7 0.0 copy-start.1
  8.7 10.6 %gather_fusion = bf16[24,512,512]{2,1,0:T(8,128)(2,1)} fusion(bf16[24,512,512]{2,1,0:T(8,128)(2,1)} %param.7, s32[1024]{0:T(1024)S(1)} %pad_clamp_fusion.1), kind=kCustom, calls=%fused_computation.2 | custom fusion | bytes 25165920 | tf_op jit(solution)/shard_map/jit(_take)/gather | solution.py:11
  19.4 0.0 copy-done
  19.4 0.0 copy-done.1
  19.4 138.6 %all-gather.7.cloned.1.call-done = bf16[1,16,512,512]{3,2,1,0:T(8,128)(2,1)} async-done(((bf16[1,16,16,512]{3,2,1,0:T(8,128)(2,1)}), bf16[1,16,512,512]{3,2,1,0:T(8,128)(2,1)}) %all-gather.7.cloned.1.call-update) | async-done | bytes 8388624 | tf_op jit(solution)/shard_map/all_gather | solution.py:14
  158.0 9.4 %gather_fusion.2 = bf16[24,512,512]{2,1,0:T(8,128)(2,1)} fusion(bf16[16,512,512]{2,1,0:T(8,128)(2,1)} %bitcast.14, s32[1024]{0:T(1024)S(1)} %get-tuple-element.12), kind=kCustom, calls=%fused_computation.1.clone | custom fusion | bytes 25165920 | tf_op jit(solution)/shard_map/jit(_take)/gather | solution.py:14
  167.4 158.9 %all-gather.5.cloned.1.call-done = bf16[1,16,512,512]{3,2,1,0:T(8,128)(2,1)} async-done(((bf16[1,16,16,512]{3,2,1,0:T(8,128)(2,1)}), bf16[1,16,512,512]{3,2,1,0:T(8,128)(2,1)}) %all-gather.5.cloned.1.call-update) | async-done | bytes 8388624 | tf_op jit(solution)/shard_map/all_gather | solution.py:18
  326.3 9.5 %gather_fusion.1 = bf16[24,512,512]{2,1,0:T(8,128)(2,1)} fusion(bf16[16,512,512]{2,1,0:T(8,128)(2,1)} %bitcast.15, s32[1024]{0:T(1024)S(1)} %get-tuple-element.13), kind=kCustom, calls=%fused_computation.clone | custom fusion | bytes 25165920 | tf_op jit(solution)/shard_map/jit(_take)/gather | solution.py:18
  335.7 21.7 %fusion.19 = bf16[24,512,512]{2,1,0:T(8,128)(2,1)} fusion(bf16[24,512,512]{2,1,0:T(8,128)(2,1)} %gather_fusion.2, bf16[24,512,512]{2,1,0:T(8,128)(2,1)} %gather_fusion, pred[24]{0:T(512)(128)(4,1)S(1)} %get-tuple-element.10, pred[24]{0:T(512)(128)(4,1)S(1)} %compare_and_fusion.2, bf16[24,512,512]{2,1,0:T(8,128)(2,1)} %gather_fusion.1, ...), kind=kOutput, calls=%fused_computation.12 | convolution fusion | flops 12916359168 | bytes 50331720 | tf_op jit(solution)/shard_map/kij,kjl->kil/dot_general | solution.py:19
  357.4 0.0 all-reduce.2.cloned.1.call-update
  357.5 249.4 %all-reduce.2.cloned.1.call-done = bf16[24,512,512]{2,1,0:T(8,128)(2,1)} async-done(((bf16[24,512,512]{2,1,0:T(8,128)(2,1)}), bf16[24,512,512]{2,1,0:T(8,128)(2,1)}) %all-reduce.2.cloned.1.call-update) | async-done | bytes 12582928 | tf_op jit(solution)/shard_map/psum | solution.py:21
  606.9 3.9 convert_convert_fusion
  (4 shorter events, 0.0 us)
Async XLA Ops:
  6.5 151.4 %all-gather.7.cloned.1.call-start = ((), (), s32[]{:S(2)}) async-start(), calls=%async_computation.2 | async-start | bytes 8650752 | tf_op jit(solution)/shard_map/all_gather | solution.py:14
  7.3 319.0 %all-gather.5.cloned.1.call-start = ((), (), s32[]{:S(2)}) async-start(), calls=%async_computation.1 | async-start | bytes 8650752 | tf_op jit(solution)/shard_map/all_gather | solution.py:18
  8.0 598.9 %all-reduce.2.cloned.1.call-start = ((), (), s32[]{:S(2)}) async-start(), calls=%async_computation | async-start | bytes 25165824 | tf_op jit(solution)/shard_map/psum | solution.py:21
  8.7 10.6 %copy-start = (s32[24,2]{0,1:T(2,128)S(1)}, s32[24,2]{0,1:T(2,128)}, u32[]{:S(2)}) copy-start(s32[24,2]{0,1:T(2,128)} %param.8) | copy-start | bytes 580
  8.7 10.6 %copy-start.1 = (s32[1,24]{1,0:T(1,128)S(1)}, s32[1,24]{1,0:T(1,128)}, u32[]{:S(2)}) copy-start(s32[1,24]{1,0:T(1,128)} %param.9) | copy-start | bytes 292
Sparse Core Ops, SparseCore 0:
  9.0 148.9 all-gather.6
  159.6 166.6 all-gather.4
  357.6 249.2 all-reduce.1
where the time goes:
time: 618 us; the launch traced here: 617 us
  waiting for transfers between devices  548 us (89%)
  local copies, waits for them, and re-layouts  29.5 us (5%)
  matrix products  21.7 us (4%)
  between operations  13.2 us (2%)
    psum x1, waiting for transfers between devices, body(): summed = lax.psum(term_out.astype(jnp.bfloat16), 'term').astype(jnp.float32)  249 us
    all_gather x1, waiting for transfers between devices, body(): lax.all_gather(left_env[0], 'sec', axis=1, tiled=True)  159 us
    all_gather x1, waiting for transfers between devices, body(): lax.all_gather(right_env[0], 'sec', axis=1, tiled=True)  139 us
    dot_general x1, matrix products, body(): jnp.einsum('kij,kjl->kil', chosen, half, preferred_element_type=jnp.float32)  21.7 us
  transfers between devices with their start and end apart: 3, of which 3 were waited for; matrix products, arithmetic and copies ran while one was open for 3% of the time, Pallas kernels for 0%

commit v1 on v0

v1 whole, which is shorter than its diff:
```python
import jax
import jax.numpy as jnp
from jax import lax
from jax.sharding import Mesh, PartitionSpec as P

SEC = ("xl", "z", "y")
TERM = ("xh", "core")


def ring4(x, ax):
    fwd = [(i, (i + 1) % 4) for i in range(4)]
    bwd = [(i, (i - 1) % 4) for i in range(4)]
    from_prev = lax.ppermute(x, ax, fwd)
    from_next = lax.ppermute(x, ax, bwd)
    h = x.shape[0] // 2
    first = lax.ppermute(from_prev[:h], ax, fwd)
    second = lax.ppermute(from_next[h:], ax, bwd)
    me = lax.axis_index(ax)
    rel = [x, from_next, jnp.concatenate([first, second]), from_prev]
    buf = jnp.zeros((4,) + x.shape, x.dtype)
    for k in range(4):
        buf = lax.dynamic_update_index_in_dim(buf, rel[k], (me + k) % 4, 0)
    return buf


def gather_envs(left, right):
    env = jnp.concatenate([left, right], axis=0)
    other = lax.ppermute(env, "xl", [(0, 1), (1, 0)])
    low = lax.axis_index("xl") == 0
    pair = jnp.where(low, jnp.stack([env, other]), jnp.stack([other, env]))
    nsec = left.shape[0]
    by_y = ring4(pair[:, :nsec], "y")
    by_z = ring4(pair[:, nsec:], "z")
    by_y = ring4(by_y, "z")
    by_z = ring4(by_z, "y")
    width = left.shape[-1]
    left_all = jnp.transpose(by_y, (3, 2, 0, 1, 4, 5)).reshape(nsec, width, width)
    right_all = jnp.transpose(by_z, (3, 2, 1, 0, 4, 5)).reshape(nsec, width, width)
    return left_all, right_all


def body(psi_tiles, sectors, sources, left_env, right_env):
    tile_count = psi_tiles.shape[0]
    width = psi_tiles.shape[2]
    local_ids = sources[0] - lax.axis_index(SEC) * tile_count
    left_all, right_all = gather_envs(left_env[0], right_env[0])
    moved = jnp.take(psi_tiles, local_ids, axis=0)
    chosen = jnp.take(right_all, sectors[:, 1], axis=0)
    half = jnp.einsum("kij,kjl->kil", moved, chosen, preferred_element_type=jnp.float32).astype(jnp.bfloat16)
    chosen = jnp.take(left_all, sectors[:, 0], axis=0)
    out = jnp.einsum("kij,kjl->kil", chosen, half, preferred_element_type=jnp.float32).astype(jnp.bfloat16)
    rows = width // 4
    xh = lax.axis_index("xh")
    core = lax.axis_index("core")
    quarter = lambda hi, c: lax.dynamic_slice_in_dim(out, (2 * hi + c) * rows, rows, 1)
    mine = quarter(xh, core)
    to_sibling = jnp.stack([quarter(xh, 1 - core), quarter(1 - xh, 1 - core)])
    from_sibling = lax.ppermute(to_sibling, "core", [(0, 1), (1, 0)])
    partial = (quarter(1 - xh, core).astype(jnp.float32) + from_sibling[1].astype(jnp.float32)).astype(jnp.bfloat16)
    remote = lax.ppermute(partial, "xh", [(0, 1), (1, 0)])
    total = mine.astype(jnp.float32) + from_sibling[0].astype(jnp.float32) + remote.astype(jnp.float32)
    return total.astype(jnp.bfloat16)


def solution(mesh):
    fine = Mesh(mesh.devices.reshape(2, 2, 2, 4, 4), TERM + SEC)
    placed = (
        P(SEC, None, None),
        P(SEC, None),
        P(TERM, SEC),
        P(TERM, None, SEC, None),
        P(TERM, None, SEC, None),
    )
    return jax.shard_map(body, mesh=fine, in_specs=placed, out_specs=P(SEC, TERM, None), check_vma=False)
```

time: 618 us -> 280 us (0.45)
  waiting for transfers between devices: 548 us -> 127 us
  local copies, waits for them, and re-layouts: 29.5 us -> 77.2 us
  starting transfers between devices: 0.08 us -> 32.8 us
  other arithmetic: 4.55 us -> 20.1 us
  between operations: 13.2 us -> 0.24 us
    all_gather x2 -> x0, waiting for transfers between devices: 297 us -> none  [the longest x1 159 us: body(): lax.all_gather(left_env[0], 'sec', axis=1, tiled=True)]
    psum x1 -> x0, waiting for transfers between devices: 249 us -> none  [body(): summed = lax.psum(term_out.astype(jnp.bfloat16), 'term').astype(jnp.float32)]
    ppermute x0 -> x19, waiting for transfers between devices: none -> 127 us  [the longest x1 68.3 us: body(): remote = lax.ppermute(partial, 'xh', [(0, 1), (1, 0)])]
    ppermute x0 -> x19, starting transfers between devices: none -> 32.8 us  [the longest x4 9.9 us: ring4(): second = lax.ppermute(from_next[h:], ax, bwd)]
    dynamic_update_slice x0 -> x12, local copies, waits for them, and re-layouts: none -> 21.4 us  [ring4(): buf = lax.dynamic_update_index_in_dim(buf, rel[k], (me + k) % 4, 0)]
    another operation x0 -> x5, local copies, waits for them, and re-layouts: none -> 10.8 us
    transpose x0 -> x1, local copies, waits for them, and re-layouts: none -> 8.13 us  [gather_envs(): jnp.transpose(by_z, (3, 2, 1, 0, 4, 5)).reshape(nsec, width, width)]
    convert_element_type x1 -> x2, other arithmetic: 3.86 us -> 11.7 us  [the longest x1 6.08 us: body(): return total.astype(jnp.bfloat16)]
  transfers between devices with their start and end apart: 3 -> 19, of which waited for: 3 -> 5; matrix products, arithmetic and copies ran while one was open for 3% -> 19% of each run, Pallas kernels for 0% -> 0%
where the time goes in v1:
time: 280 us; the launch traced here: 279 us
  waiting for transfers between devices  127 us (45%)
  local copies, waits for them, and re-layouts  77.2 us (28%)
  starting transfers between devices  32.8 us (12%)
  matrix products  21.8 us (8%)
  other arithmetic  20.1 us (7%)
    ppermute x1, waiting for transfers between devices, body(): remote = lax.ppermute(partial, 'xh', [(0, 1), (1, 0)])  68.3 us
    ppermute x4, waiting for transfers between devices, ring4(): from_prev = lax.ppermute(x, ax, fwd)  37.4 us
    dot_general x1, matrix products, body(): jnp.einsum('kij,kjl->kil', chosen, half, preferred_element_type=jnp.float32)  21.8 us
    dynamic_update_slice x12, local copies, waits for them, and re-layouts, ring4(): buf = lax.dynamic_update_index_in_dim(buf, rel[k], (me + k) % 4, 0)  21.4 us
    ppermute x1, waiting for transfers between devices, gather_envs(): other = lax.ppermute(env, 'xl', [(0, 1), (1, 0)])  11.2 us
    gather x1, local copies, waits for them, and re-layouts, body(): moved = jnp.take(psi_tiles, local_ids, axis=0)  10.6 us
    ppermute x1, waiting for transfers between devices, body(): from_sibling = lax.ppermute(to_sibling, 'core', [(0, 1), (1, 0)])  10.1 us
    ppermute x4, starting transfers between devices, ring4(): second = lax.ppermute(from_next[h:], ax, bwd)  9.9 us
  transfers between devices with their start and end apart: 19, of which 5 were waited for; matrix products, arithmetic and copies ran while one was open for 19% of the time, Pallas kernels for 0%

profile of v1, /device:TPU:1, one launch (start us, length us, event | category | flops | bytes accessed | tf_op | source)
XLA Modules:
  0.0 279.2 jit_solution(8581544773321885736)
XLA Ops:
  1.1 2.1 collective-permute-start
  3.2 11.2 %collective-permute-done = bf16[32,16,512]{2,1,0:T(8,128)(2,1)S(1)} collective-permute-done((bf16[32,16,512]{2,1,0:T(8,128)(2,1)S(1)}, bf16[32,16,512]{2,1,0:T(8,128)(2,1)S(1)}, u32[]{:S(2)}, u32[]{:S(2)}) %collective-permute-start) | collective-permute-done | bytes 524320 | tf_op jit(solution)/shard_map/ppermute | solution.py:28
  15.6 2.0 collective-permute-start.10
  17.6 2.1 collective-permute-start.9
  22.5 8.2 %collective-permute-done.10 = bf16[2,16,16,512]{3,2,0,1:T(8,128)(2,1)S(1)} collective-permute-done((bf16[2,16,16,512]{3,2,0,1:T(8,128)(2,1)}, bf16[2,16,16,512]{3,2,0,1:T(8,128)(2,1)S(1)}, u32[]{:S(2)}, u32[]{:S(2)}) %collective-permute-start.10) | collective-permute-done | bytes 524320 | tf_op jit(solution)/shard_map/ppermute | solution.py:13
  30.8 2.7 collective-permute-start.12
  33.6 1.6 broadcast.73.clone
  45.6 2.7 collective-permute-start.5
  48.3 10.6 %gather_fusion = bf16[24,512,512]{2,1,0:T(8,128)(2,1)} fusion(bf16[24,512,512]{2,1,0:T(8,128)(2,1)} %param.7, s32[1024]{0:T(1024)S(1)} %pad_clamp_fusion.1), kind=kCustom, calls=%fused_computation.2 | custom fusion | bytes 25165920 | tf_op jit(solution)/shard_map/jit(_take)/gather | solution.py:47
  58.9 29.1 %collective-permute-done.14 = bf16[4,2,16,16,512]{4,3,0,1,2:T(8,128)(2,1)} collective-permute-done((bf16[4,2,16,16,512]{4,3,0,1,2:T(8,128)(2,1)}, bf16[4,2,16,16,512]{4,3,0,1,2:T(8,128)(2,1)}, u32[]{:S(2)}, u32[]{:S(2)}) %collective-permute-start.14) | collective-permute-done | bytes 2097184 | tf_op jit(solution)/shard_map/ppermute | solution.py:13
  90.9 2.7 collective-permute-start.16
  94.9 4.3 %broadcast.72.clone = bf16[4,4,2,16,16,512]{5,4,1,0,2,3:T(8,128)(2,1)} broadcast(bf16[]{:T(256)} %constant.137.clone.1), dimensions={} | broadcast | bytes 8388610 | tf_op jit(solution)/shard_map/broadcast.18
  99.3 3.3 %bitcast_dynamic-update-slice_fusion.2 = bf16[4,4,2,16,16,512]{5,4,1,0,2,3:T(8,128)(2,1)} fusion(bf16[4,4,2,16,16,512]{5,4,1,0,2,3:T(8,128)(2,1)} %broadcast.72.clone, s32[]{:T(128)S(6)} %select_n.134, bf16[4,2,16,16,512]{4,3,0,1,2:T(8,128)(2,1)} %bitcast_dynamic-update-slice_fusion.6), kind=kLoop, calls=%fused_computation.30 | loop fusion | bytes 4194308 | tf_op jit(solution)/shard_map/jit(dynamic_update_index_in_dim)/dynamic_update_slice | solution.py:22
  102.5 2.3 slice.65
  106.2 2.9 %collective-permute-start.8 = (bf16[2,2,16,16,512]{4,3,0,1,2:T(8,128)(2,1)S(1)}, bf16[2,2,16,16,512]{4,3,0,1,2:T(8,128)(2,1)S(1)}, u32[]{:S(2)}, u32[]{:S(2)}) collective-permute-start(bf16[2,2,16,16,512]{4,3,0,1,2:T(8,128)(2,1)S(1)} %slice.66), channel_id=1, source_target_pairs={{0,12},{4,0},{8,4},{12,8},{1,13},{5,1},{9,5},{13,9},{2,14},{6,2},{... | collective-permute-start | bytes 3145736 | tf_op jit(solution)/shard_map/ppermute | solution.py:17
  109.1 1.9 bitcast_dynamic-update-slice_fusion.3
  111.0 4.8 %bitcast_dynamic-update-slice_fusion.1 = bf16[4,4,2,16,16,512]{5,4,1,0,2,3:T(8,128)(2,1)} fusion(bf16[4,4,2,16,16,512]{5,4,1,0,2,3:T(8,128)(2,1)} %bitcast_dynamic-update-slice_fusion.2, s32[]{:T(128)S(6)} %select_n.136, bf16[4,2,16,16,512]{4,3,0,1,2:T(8,128)(2,1)} %collective-permute-done.13), kind=kLoop, calls=%fused_computation.29 | loop fusion | bytes 4194308 | tf_op jit(solution)/shard_map/jit(dynamic_update_index_in_dim)/dynamic_update_slice | solution.py:22
  117.3 3.2 %bitcast_dynamic-update-slice_fusion = bf16[4,4,2,16,16,512]{5,4,1,0,2,3:T(8,128)(2,1)} fusion(bf16[4,4,2,16,16,512]{5,4,1,0,2,3:T(8,128)(2,1)} %fusion.34, s32[]{:T(128)S(6)} %select_n.140, bf16[4,2,16,16,512]{4,3,0,1,2:T(8,128)(2,1)} %collective-permute-done.14), kind=kLoop, calls=%fused_computation.28 | loop fusion | bytes 4194308 | tf_op jit(solution)/shard_map/jit(dynamic_update_index_in_dim)/dynamic_update_slice | solution.py:22
  120.6 8.1 %copy.20 = bf16[16,2,4,4,16,512]{5,4,3,2,1,0:T(8,128)(2,1)} copy(bf16[16,2,4,4,16,512]{5,4,2,3,1,0:T(8,128)(2,1)} %bitcast.41) | data formatting | bytes 16777216 | tf_op jit(solution)/shard_map/transpose | solution.py:38
  128.7 1.6 fusion.33
  130.3 3.2 %bitcast_dynamic-update-slice_fusion.5 = bf16[4,4,2,16,16,512]{5,4,1,0,2,3:T(8,128)(2,1)} fusion(bf16[4,4,2,16,16,512]{5,4,1,0,2,3:T(8,128)(2,1)} %fusion.33, s32[]{:T(128)S(6)} %select_n.148, bf16[4,2,16,16,512]{4,3,0,1,2:T(8,128)(2,1)} %collective-permute-done.6), kind=kLoop, calls=%fused_computation.33 | loop fusion | bytes 4194308 | tf_op jit(solution)/shard_map/jit(dynamic_update_index_in_dim)/dynamic_update_slice | solution.py:22
  133.5 9.5 %gather_fusion.1 = bf16[24,512,512]{2,1,0:T(8,128)(2,1)} fusion(bf16[16,512,512]{2,1,0:T(8,128)(2,1)} %bitcast.105, s32[1024]{0:T(1024)S(1)} %get-tuple-element.19), kind=kCustom, calls=%fused_computation.clone | custom fusion | bytes 25165920 | tf_op jit(solution)/shard_map/jit(_take)/gather | solution.py:50
  143.0 9.3 %gather_fusion.2 = bf16[24,512,512]{2,1,0:T(8,128)(2,1)} fusion(bf16[16,512,512]{2,1,0:T(8,128)(2,1)} %bitcast.104, s32[1024]{0:T(1024)S(1)} %get-tuple-element.18), kind=kCustom, calls=%fused_computation.1.clone | custom fusion | bytes 25165920 | tf_op jit(solution)/shard_map/jit(_take)/gather | solution.py:48
  152.3 21.8 %fusion.19 = bf16[24,512,512]{2,1,0:T(8,128)(2,1)} fusion(bf16[24,512,512]{2,1,0:T(8,128)(2,1)} %gather_fusion.2, bf16[24,512,512]{2,1,0:T(8,128)(2,1)} %gather_fusion, pred[24]{0:T(512)(128)(4,1)S(1)} %get-tuple-element.16, pred[24]{0:T(512)(128)(4,1)S(1)} %compare_and_fusion.2, bf16[24,512,512]{2,1,0:T(8,128)(2,1)} %gather_fusion.1, ...), kind=kOutput, calls=%fused_computation.12 | convolution fusion | flops 12916359168 | bytes 50331720 | tf_op jit(solution)/shard_map/kij,kjl->kil/dot_general | solution.py:51
  174.1 3.6 %dynamic-slice_bitcast_fusion.1 = (bf16[1,24,128,512]{3,2,1,0:T(8,128)(2,1)S(1)}, bf16[1,24,128,512]{3,2,1,0:T(8,128)(2,1)S(1)}) fusion(bf16[24,512,512]{2,1,0:T(8,128)(2,1)} %fusion.19, s32[]{:T(128)S(6)} %select_n.153, s32[]{:T(128)S(6)} %select_n.154), kind=kLoop, calls=%fused_computation.23 | loop fusion | bytes 12582920 | tf_op jit(solution)/shard_map/stack | solution.py:57
  177.7 3.2 %pad_maximum_fusion = bf16[2,24,128,512]{3,2,1,0:T(8,128)(2,1)} fusion(bf16[1,24,128,512]{3,2,1,0:T(8,128)(2,1)S(1)} %get-tuple-element.11, bf16[1,24,128,512]{3,2,1,0:T(8,128)(2,1)S(1)} %get-tuple-element.10), kind=kLoop, calls=%fused_computation.13 | loop fusion | flops 3145728 | bytes 12582912 | tf_op jit(solution)/shard_map/stack | solution.py:57
  180.8 5.5 %collective-permute-start.17 = (bf16[2,24,128,512]{3,2,1,0:T(8,128)(2,1)}, bf16[2,24,128,512]{3,2,1,0:T(8,128)(2,1)}, u32[]{:S(2)}, u32[]{:S(2)}) collective-permute-start(bf16[2,24,128,512]{3,2,1,0:T(8,128)(2,1)} %pad_maximum_fusion), channel_id=1, source_target_pairs={{0,32},{32,0},{1,33},{33,1},{2,34},{34,2},{3,35},{35,3},{4,36},{36... | collective-permute-start | bytes 18874376 | tf_op jit(solution)/shard_map/ppermute | solution.py:58
  186.3 10.1 %collective-permute-done.17 = bf16[2,24,128,512]{3,2,1,0:T(8,128)(2,1)} collective-permute-done((bf16[2,24,128,512]{3,2,1,0:T(8,128)(2,1)}, bf16[2,24,128,512]{3,2,1,0:T(8,128)(2,1)}, u32[]{:S(2)}, u32[]{:S(2)}) %collective-permute-start.17) | collective-permute-done | bytes 6291488 | tf_op jit(solution)/shard_map/ppermute | solution.py:58
  196.4 5.7 %fusion.28 = bf16[24,128,512]{2,1,0:T(8,128)(2,1)} fusion(bf16[2,24,128,512]{3,2,1,0:T(8,128)(2,1)} %collective-permute-done.17, bf16[24,512,512]{2,1,0:T(8,128)(2,1)} %fusion.19, s32[]{:T(128)S(6)} %select_n.155), kind=kLoop, calls=%fused_computation.15 | loop fusion | flops 6291456 | bytes 9437188 | tf_op jit(solution)/shard_map/convert_element_type | solution.py:59
  202.1 2.7 collective-permute-start.18
  204.8 68.3 %collective-permute-done.18 = bf16[24,128,512]{2,1,0:T(8,128)(2,1)S(1)} collective-permute-done((bf16[24,128,512]{2,1,0:T(8,128)(2,1)}, bf16[24,128,512]{2,1,0:T(8,128)(2,1)S(1)}, u32[]{:S(2)}, u32[]{:S(2)}) %collective-permute-start.18) | collective-permute-done | bytes 3145760 | tf_op jit(solution)/shard_map/ppermute | solution.py:60
  273.1 6.1 %fusion.30 = bf16[24,128,512]{2,1,0:T(8,128)(2,1)} fusion(bf16[24,128,512]{2,1,0:T(8,128)(2,1)S(1)} %collective-permute-done.18, bf16[2,24,128,512]{3,2,1,0:T(8,128)(2,1)} %collective-permute-done.17, bf16[24,512,512]{2,1,0:T(8,128)(2,1)} %fusion.19, s32[]{:T(128)S(6)} %select_n.152), kind=kLoop, calls=%fused_computation.18 | loop fusion | flops 9437184 | bytes 12582916 | tf_op jit(solution)/shard_map/convert_element_type | solution.py:62
  (61 shorter events, 22.4 us)
Async XLA Ops:
  1.1 13.3 %collective-permute-start = (bf16[32,16,512]{2,1,0:T(8,128)(2,1)S(1)}, bf16[32,16,512]{2,1,0:T(8,128)(2,1)S(1)}, u32[]{:S(2)}, u32[]{:S(2)}) collective-permute-start(bf16[32,16,512]{2,1,0:T(8,128)(2,1)S(1)} %get-tuple-element.15), channel_id=1, source_target_pairs={{0,16},{16,0},{1,17},{17,1},{2,18},{18,2},{3,19},{19,3},{4,20},{20... | collective-permute-start | bytes 1572872 | tf_op jit(solution)/shard_map/ppermute | solution.py:28
  15.6 15.1 %collective-permute-start.10 = (bf16[2,16,16,512]{3,2,0,1:T(8,128)(2,1)}, bf16[2,16,16,512]{3,2,0,1:T(8,128)(2,1)S(1)}, u32[]{:S(2)}, u32[]{:S(2)}) collective-permute-start(bf16[2,16,16,512]{3,2,0,1:T(8,128)(2,1)} %get-tuple-element.13), channel_id=1, source_target_pairs={{0,4},{4,8},{8,12},{12,0},{1,5},{5,9},{9,13},{13,1},{2,6},{6,10},{... | collective-permute-start | bytes 1572872 | tf_op jit(solution)/shard_map/ppermute | solution.py:13
  17.6 13.2 %collective-permute-start.9 = (bf16[2,16,16,512]{3,2,0,1:T(8,128)(2,1)}, bf16[2,16,16,512]{3,2,0,1:T(8,128)(2,1)S(1)}, u32[]{:S(2)}, u32[]{:S(2)}) collective-permute-start(bf16[2,16,16,512]{3,2,0,1:T(8,128)(2,1)} %get-tuple-element.13), channel_id=1, source_target_pairs={{0,12},{4,0},{8,4},{12,8},{1,13},{5,1},{9,5},{13,9},{2,14},{6,2},{... | collective-permute-start | bytes 1572872 | tf_op jit(solution)/shard_map/ppermute | solution.py:14
  19.7 16.3 %collective-permute-start.2 = (bf16[2,16,16,512]{3,2,0,1:T(8,128)(2,1)}, bf16[2,16,16,512]{3,2,0,1:T(8,128)(2,1)S(1)}, u32[]{:S(2)}, u32[]{:S(2)}) collective-permute-start(bf16[2,16,16,512]{3,2,0,1:T(8,128)(2,1)} %get-tuple-element.12), channel_id=1, source_target_pairs={{0,1},{1,2},{2,3},{3,0},{4,5},{5,6},{6,7},{7,4},{8,9},{9,10},{10,1... | collective-permute-start | bytes 1572872 | tf_op jit(solution)/shard_map/ppermute | solution.py:13
  21.0 16.4 %collective-permute-start.1 = (bf16[2,16,16,512]{3,2,0,1:T(8,128)(2,1)}, bf16[2,16,16,512]{3,2,0,1:T(8,128)(2,1)S(1)}, u32[]{:S(2)}, u32[]{:S(2)}) collective-permute-start(bf16[2,16,16,512]{3,2,0,1:T(8,128)(2,1)} %get-tuple-element.12), channel_id=1, source_target_pairs={{0,3},{1,0},{2,1},{3,2},{4,7},{5,4},{6,5},{7,6},{8,11},{9,8},{10,9... | collective-permute-start | bytes 1572872 | tf_op jit(solution)/shard_map/ppermute | solution.py:14
  30.7 9.1 %collective-permute-start.11 = (bf16[1,16,16,512]{3,2,0,1:T(8,128)(2,1)S(1)}, bf16[1,16,16,512]{3,2,0,1:T(8,128)(2,1)S(1)}, u32[]{:S(2)}, u32[]{:S(2)}) collective-permute-start(bf16[1,16,16,512]{3,2,0,1:T(8,128)(2,1)S(1)} %slice.68), channel_id=1, source_target_pairs={{0,4},{4,8},{8,12},{12,0},{1,5},{5,9},{9,13},{13,1},{2,6},{6,10},{... | collective-permute-start | bytes 786440 | tf_op jit(solution)/shard_map/ppermute | solution.py:16
  30.8 8.9 %collective-permute-start.12 = (bf16[1,16,16,512]{3,2,0,1:T(8,128)(2,1)S(1)}, bf16[1,16,16,512]{3,2,0,1:T(8,128)(2,1)S(1)}, u32[]{:S(2)}, u32[]{:S(2)}) collective-permute-start(bf16[1,16,16,512]{3,2,0,1:T(8,128)(2,1)S(1)} %slice.69), channel_id=1, source_target_pairs={{0,12},{4,0},{8,4},{12,8},{1,13},{5,1},{9,5},{13,9},{2,14},{6,2},{... | collective-permute-start | bytes 786440 | tf_op jit(solution)/shard_map/ppermute | solution.py:17
  35.1 13.1 %copy-start.4 = (s32[1,24]{1,0:T(1,128)S(1)}, s32[1,24]{1,0:T(1,128)}, u32[]{:S(2)}) copy-start(s32[1,24]{1,0:T(1,128)} %param.9) | copy-start | bytes 292
  36.0 6.9 %copy-start.1 = (bf16[2,16,16,512]{3,2,0,1:T(8,128)(2,1)}, bf16[2,16,16,512]{3,2,0,1:T(8,128)(2,1)S(1)}, u32[]{:S(2)}) copy-start(bf16[2,16,16,512]{3,2,0,1:T(8,128)(2,1)S(1)} %collective-permute-done.2) | copy-start | bytes 1572868
  36.0 8.3 %collective-permute-start.3 = (bf16[1,16,16,512]{3,2,0,1:T(8,128)(2,1)S(1)}, bf16[1,16,16,512]{3,2,0,1:T(8,128)(2,1)S(1)}, u32[]{:S(2)}, u32[]{:S(2)}) collective-permute-start(bf16[1,16,16,512]{3,2,0,1:T(8,128)(2,1)S(1)} %slice.63), channel_id=1, source_target_pairs={{0,1},{1,2},{2,3},{3,0},{4,5},{5,6},{6,7},{7,4},{8,9},{9,10},{10,1... | collective-permute-start | bytes 786440 | tf_op jit(solution)/shard_map/ppermute | solution.py:16
  37.4 5.5 %copy-start.2 = (bf16[2,16,16,512]{3,2,0,1:T(8,128)(2,1)}, bf16[2,16,16,512]{3,2,0,1:T(8,128)(2,1)S(1)}, u32[]{:S(2)}) copy-start(bf16[2,16,16,512]{3,2,0,1:T(8,128)(2,1)S(1)} %collective-permute-done.1) | copy-start | bytes 1572868
  37.4 6.9 %collective-permute-start.4 = (bf16[1,16,16,512]{3,2,0,1:T(8,128)(2,1)S(1)}, bf16[1,16,16,512]{3,2,0,1:T(8,128)(2,1)S(1)}, u32[]{:S(2)}, u32[]{:S(2)}) collective-permute-start(bf16[1,16,16,512]{3,2,0,1:T(8,128)(2,1)S(1)} %slice.64), channel_id=1, source_target_pairs={{0,3},{1,0},{2,1},{3,2},{4,7},{5,4},{6,5},{7,6},{8,11},{9,8},{10,9... | collective-permute-start | bytes 786440 | tf_op jit(solution)/shard_map/ppermute | solution.py:17
  41.4 48.1 %collective-permute-start.13 = (bf16[4,2,16,16,512]{4,3,0,1,2:T(8,128)(2,1)}, bf16[4,2,16,16,512]{4,3,0,1,2:T(8,128)(2,1)}, u32[]{:S(2)}, u32[]{:S(2)}) collective-permute-start(bf16[4,2,16,16,512]{4,3,0,1,2:T(8,128)(2,1)} %bitcast_dynamic-update-slice_fusion.6), channel_id=1, source_target_pairs={{0,3},{1,0},{2,1},{3,2},{4,7},{5,4},{6,5},{7,6},{8,11},{9,8},{10,9... | collective-permute-start | bytes 6291464 | tf_op jit(solution)/shard_map/ppermute | solution.py:14
  42.9 45.2 %collective-permute-start.14 = (bf16[4,2,16,16,512]{4,3,0,1,2:T(8,128)(2,1)}, bf16[4,2,16,16,512]{4,3,0,1,2:T(8,128)(2,1)}, u32[]{:S(2)}, u32[]{:S(2)}) collective-permute-start(bf16[4,2,16,16,512]{4,3,0,1,2:T(8,128)(2,1)} %bitcast_dynamic-update-slice_fusion.6), channel_id=1, source_target_pairs={{0,1},{1,2},{2,3},{3,0},{4,5},{5,6},{6,7},{7,4},{8,9},{9,10},{10,1... | collective-permute-start | bytes 6291464 | tf_op jit(solution)/shard_map/ppermute | solution.py:13
  45.5 57.1 %collective-permute-start.6 = (bf16[4,2,16,16,512]{4,3,0,1,2:T(8,128)(2,1)S(1)}, bf16[4,2,16,16,512]{4,3,0,1,2:T(8,128)(2,1)}, u32[]{:S(2)}, u32[]{:S(2)}) collective-permute-start(bf16[4,2,16,16,512]{4,3,0,1,2:T(8,128)(2,1)S(1)} %bitcast_dynamic-update-slice_fusion.11), channel_id=1, source_target_pairs={{0,4},{4,8},{8,12},{12,0},{1,5},{5,9},{9,13},{13,1},{2,6},{6,10},{... | collective-permute-start | bytes 6291464 | tf_op jit(solution)/shard_map/ppermute | solution.py:13
  45.6 59.3 %collective-permute-start.5 = (bf16[4,2,16,16,512]{4,3,0,1,2:T(8,128)(2,1)S(1)}, bf16[4,2,16,16,512]{4,3,0,1,2:T(8,128)(2,1)}, u32[]{:S(2)}, u32[]{:S(2)}) collective-permute-start(bf16[4,2,16,16,512]{4,3,0,1,2:T(8,128)(2,1)S(1)} %bitcast_dynamic-update-slice_fusion.11), channel_id=1, source_target_pairs={{0,12},{4,0},{8,4},{12,8},{1,13},{5,1},{9,5},{13,9},{2,14},{6,2},{... | collective-permute-start | bytes 6291464 | tf_op jit(solution)/shard_map/ppermute | solution.py:14
  48.2 10.7 %copy-start.3 = (s32[24,2]{0,1:T(2,128)S(1)}, s32[24,2]{0,1:T(2,128)}, u32[]{:S(2)}) copy-start(s32[24,2]{0,1:T(2,128)} %param.8) | copy-start | bytes 580
  89.4 26.4 %collective-permute-start.15 = (bf16[2,2,16,16,512]{4,3,0,1,2:T(8,128)(2,1)S(1)}, bf16[2,2,16,16,512]{4,3,0,1,2:T(8,128)(2,1)S(1)}, u32[]{:S(2)}, u32[]{:S(2)}) collective-permute-start(bf16[2,2,16,16,512]{4,3,0,1,2:T(8,128)(2,1)S(1)} %slice.70), channel_id=1, source_target_pairs={{0,1},{1,2},{2,3},{3,0},{4,5},{5,6},{6,7},{7,4},{8,9},{9,10},{10,1... | collective-permute-start | bytes 3145736 | tf_op jit(solution)/shard_map/ppermute | solution.py:16
  90.9 25.0 %collective-permute-start.16 = (bf16[2,2,16,16,512]{4,3,0,1,2:T(8,128)(2,1)S(1)}, bf16[2,2,16,16,512]{4,3,0,1,2:T(8,128)(2,1)S(1)}, u32[]{:S(2)}, u32[]{:S(2)}) collective-permute-start(bf16[2,2,16,16,512]{4,3,0,1,2:T(8,128)(2,1)S(1)} %slice.71), channel_id=1, source_target_pairs={{0,3},{1,0},{2,1},{3,2},{4,7},{5,4},{6,5},{7,6},{8,11},{9,8},{10,9... | collective-permute-start | bytes 3145736 | tf_op jit(solution)/shard_map/ppermute | solution.py:17
  104.8 23.9 %collective-permute-start.7 = (bf16[2,2,16,16,512]{4,3,0,1,2:T(8,128)(2,1)}, bf16[2,2,16,16,512]{4,3,0,1,2:T(8,128)(2,1)S(1)}, u32[]{:S(2)}, u32[]{:S(2)}) collective-permute-start(bf16[2,2,16,16,512]{4,3,0,1,2:T(8,128)(2,1)} %slice.65), channel_id=1, source_target_pairs={{0,4},{4,8},{8,12},{12,0},{1,5},{5,9},{9,13},{13,1},{2,6},{6,10},{... | collective-permute-start | bytes 3145736 | tf_op jit(solution)/shard_map/ppermute | solution.py:16
  106.2 22.5 %collective-permute-start.8 = (bf16[2,2,16,16,512]{4,3,0,1,2:T(8,128)(2,1)S(1)}, bf16[2,2,16,16,512]{4,3,0,1,2:T(8,128)(2,1)S(1)}, u32[]{:S(2)}, u32[]{:S(2)}) collective-permute-start(bf16[2,2,16,16,512]{4,3,0,1,2:T(8,128)(2,1)S(1)} %slice.66), channel_id=1, source_target_pairs={{0,12},{4,0},{8,4},{12,8},{1,13},{5,1},{9,5},{13,9},{2,14},{6,2},{... | collective-permute-start | bytes 3145736 | tf_op jit(solution)/shard_map/ppermute | solution.py:17
  111.0 9.6 %copy-start = (bf16[4,4,2,16,16,512]{5,4,1,0,2,3:T(8,128)(2,1)}, bf16[4,4,2,16,16,512]{5,4,1,0,2,3:T(8,128)(2,1)S(1)}, u32[]{:S(2)}) copy-start(bf16[4,4,2,16,16,512]{5,4,1,0,2,3:T(8,128)(2,1)S(1)} %bitcast_dynamic-update-slice_fusion.3) | copy-start | bytes 25165828
  180.8 15.6 %collective-permute-start.17 = (bf16[2,24,128,512]{3,2,1,0:T(8,128)(2,1)}, bf16[2,24,128,512]{3,2,1,0:T(8,128)(2,1)}, u32[]{:S(2)}, u32[]{:S(2)}) collective-permute-start(bf16[2,24,128,512]{3,2,1,0:T(8,128)(2,1)} %pad_maximum_fusion), channel_id=1, source_target_pairs={{0,32},{32,0},{1,33},{33,1},{2,34},{34,2},{3,35},{35,3},{4,36},{36... | collective-permute-start | bytes 18874376 | tf_op jit(solution)/shard_map/ppermute | solution.py:58
  202.1 71.0 %collective-permute-start.18 = (bf16[24,128,512]{2,1,0:T(8,128)(2,1)}, bf16[24,128,512]{2,1,0:T(8,128)(2,1)S(1)}, u32[]{:S(2)}, u32[]{:S(2)}) collective-permute-start(bf16[24,128,512]{2,1,0:T(8,128)(2,1)} %fusion.28), channel_id=1, source_target_pairs={{0,64},{64,0},{1,65},{65,1},{2,66},{66,2},{3,67},{67,3},{4,68},{68... | collective-permute-start | bytes 9437192 | tf_op jit(solution)/shard_map/ppermute | solution.py:60

commit v2 on v1

v2 whole, which is shorter than its diff:
```python
import jax
import jax.numpy as jnp
from jax import lax
from jax.experimental import pallas as pl
from jax.experimental.pallas import tpu as pltpu
from jax.sharding import Mesh, PartitionSpec as P

SEC = ("xl", "z", "y")
TERM = ("xh", "core")
SWAP = [(0, 1), (1, 0)]


def ring4(x, ax, at):
    fwd = [(i, (i + 1) % 4) for i in range(4)]
    bwd = [(i, (i - 1) % 4) for i in range(4)]
    from_prev = lax.ppermute(x, ax, fwd)
    from_next = lax.ppermute(x, ax, bwd)
    h = x.shape[0] // 2
    first = lax.ppermute(from_prev[:h], ax, fwd)
    second = lax.ppermute(from_next[h:], ax, bwd)
    me = lax.axis_index(ax)
    rel = [x, from_next, jnp.concatenate([first, second]), from_prev]
    shape = x.shape[:at] + (4,) + x.shape[at:]
    buf = jnp.zeros(shape, x.dtype)
    for k in range(4):
        start = [0] * len(shape)
        start[at] = (me + k) % 4
        buf = lax.dynamic_update_slice(buf, jnp.expand_dims(rel[k], at), start)
    return buf


def plane_y(x):
    return ring4(ring4(x, "y", 0), "z", 0)


def plane_z(x):
    return ring4(ring4(x, "z", 0), "y", 1)


def first_kernel(src, s0, s1, xl, psi_own, psi_other, r_own, r_other, l_left, l_right, half_ref, out_ref):
    acc = jnp.dot(psi_own[...], r_own[...].reshape(-1, r_own.shape[-1]), preferred_element_type=jnp.float32)
    acc += jnp.dot(psi_other[...], r_other[...].reshape(-1, r_other.shape[-1]), preferred_element_type=jnp.float32)
    half = acc.astype(jnp.bfloat16)
    half_ref[...] = half
    cut = l_left.shape[-1]
    out = jnp.dot(l_left[...].reshape(-1, cut), half[:cut], preferred_element_type=jnp.float32)
    out += jnp.dot(l_right[...].reshape(-1, cut), half[cut:], preferred_element_type=jnp.float32)
    out_ref[...] = out.astype(out_ref.dtype)


def second_kernel(s0, half_ref, l_left, l_right, out_ref):
    cut = l_left.shape[-1]
    out = jnp.dot(l_left[...].reshape(-1, cut), half_ref[:cut], preferred_element_type=jnp.float32)
    out += jnp.dot(l_right[...].reshape(-1, cut), half_ref[cut:], preferred_element_type=jnp.float32)
    out_ref[...] = out.astype(out_ref.dtype)


def env_spec(shape, which):
    block = (shape[0], shape[1], None) + tuple(shape[3:])
    if which == 1:
        return pl.BlockSpec(block, lambda k, src, s0, s1, xl: (0, 0, s1[k], 0, 0))
    return pl.BlockSpec(block, lambda k, src, s0, s1, xl: (0, 0, s0[k], 0, 0))


def first_call(src, s0, s1, xl, psi, r_own, r_other, l_left, l_right):
    tiles, width, _ = psi.shape
    cut = width // 2
    grid = pltpu.PrefetchScalarGridSpec(
        num_scalar_prefetch=4,
        grid=(tiles,),
        in_specs=[
            pl.BlockSpec((None, width, cut), lambda k, src, s0, s1, xl: (src[k], 0, xl[0])),
            pl.BlockSpec((None, width, cut), lambda k, src, s0, s1, xl: (src[k], 0, 1 - xl[0])),
            env_spec(r_own.shape, 1),
            env_spec(r_other.shape, 1),
            env_spec(l_left.shape, 0),
            env_spec(l_right.shape, 0),
        ],
        out_specs=[
            pl.BlockSpec((None, width, width), lambda k, src, s0, s1, xl: (k, 0, 0)),
            pl.BlockSpec((None, cut, width), lambda k, src, s0, s1, xl: (k, 0, 0)),
        ],
    )
    flops = tiles * (2 * width**3 + 2 * cut * width * width)
    return pl.pallas_call(
        first_kernel,
        grid_spec=grid,
        out_shape=[
            jax.ShapeDtypeStruct((tiles, width, width), jnp.bfloat16),
            jax.ShapeDtypeStruct((tiles, cut, width), jnp.bfloat16),
        ],
        compiler_params=pltpu.CompilerParams(dimension_semantics=("arbitrary",)),
        cost_estimate=pl.CostEstimate(flops=flops, transcendentals=0, bytes_accessed=tiles * width * width * 2 * 4),
    )(src, s0, s1, xl, psi, psi, r_own, r_other, l_left, l_right)


def second_call(s0, half, l_left, l_right):
    tiles, width, _ = half.shape
    cut = width // 2
    block = lambda shape: pl.BlockSpec((shape[0], shape[1], None) + tuple(shape[3:]), lambda k, s0: (0, 0, s0[k], 0, 0))
    grid = pltpu.PrefetchScalarGridSpec(
        num_scalar_prefetch=1,
        grid=(tiles,),
        in_specs=[
            pl.BlockSpec((None, width, width), lambda k, s0: (k, 0, 0)),
            block(l_left.shape),
            block(l_right.shape),
        ],
        out_specs=pl.BlockSpec((None, cut, width), lambda k, s0: (k, 0, 0)),
    )
    return pl.pallas_call(
        second_kernel,
        grid_spec=grid,
        out_shape=jax.ShapeDtypeStruct((tiles, cut, width), jnp.bfloat16),
        compiler_params=pltpu.CompilerParams(dimension_semantics=("arbitrary",)),
        cost_estimate=pl.CostEstimate(flops=tiles * 2 * cut * width * width, transcendentals=0, bytes_accessed=tiles * width * width * 2 * 2),
    )(s0, half, l_left, l_right)


def body(psi_tiles, sectors, sources, left_env, right_env):
    tile_count, width, _ = psi_tiles.shape
    cut = width // 2
    xh = lax.axis_index("xh")
    core = lax.axis_index("core")
    xl = lax.axis_index("xl")
    left, right = left_env[0], right_env[0]
    r_own = plane_y(right)
    pair = lax.ppermute(jnp.stack([left, right]), "xl", SWAP)
    left_other, r_other_piece = pair[0], pair[1]
    r_other = plane_z(r_other_piece)
    own_is_early = xl != xh
    l_early = jnp.where(own_is_early, left, left_other)
    l_late = jnp.where(own_is_early, left_other, left)
    early_left = plane_y(l_early[..., :cut])
    early_right = plane_z(l_early[..., cut:])
    src = (sources[0] - lax.axis_index(SEC) * tile_count).astype(jnp.int32)
    s0 = sectors[:, 0].astype(jnp.int32)
    s1 = sectors[:, 1].astype(jnp.int32)
    half, out_rem = first_call(src, s0, s1, xl.reshape(1).astype(jnp.int32), psi_tiles, r_own, r_other, early_left, early_right)
    rows = width // 4
    mine_rem = lax.dynamic_slice_in_dim(out_rem, core * rows, rows, 1)
    to_sib = lax.dynamic_slice_in_dim(out_rem, (1 - core) * rows, rows, 1)
    from_sib = lax.ppermute(to_sib, "core", SWAP)
    partial = (mine_rem.astype(jnp.float32) + from_sib.astype(jnp.float32)).astype(jnp.bfloat16)
    remote = lax.ppermute(partial, "xh", SWAP)
    late_left = plane_y(l_late[..., :cut])
    late_right = plane_z(l_late[..., cut:])
    out_loc = second_call(s0, half, late_left, late_right)
    mine_loc = lax.dynamic_slice_in_dim(out_loc, core * rows, rows, 1)
    to_sib2 = lax.dynamic_slice_in_dim(out_loc, (1 - core) * rows, rows, 1)
    from_sib2 = lax.ppermute(to_sib2, "core", SWAP)
    total = mine_loc.astype(jnp.float32) + from_sib2.astype(jnp.float32) + remote.astype(jnp.float32)
    return total.astype(jnp.bfloat16)


def solution(mesh):
    fine = Mesh(mesh.devices.reshape(2, 2, 2, 4, 4), TERM + SEC)
    placed = (
        P(SEC, None, None),
        P(SEC, None),
        P(TERM, SEC),
        P(TERM, None, SEC, None),
        P(TERM, None, SEC, None),
    )
    return jax.shard_map(body, mesh=fine, in_specs=placed, out_specs=P(SEC, TERM, None), check_vma=False)
```

time: 280 us -> 319 us (1.14)
  local copies, waits for them, and re-layouts: 77.2 us -> 26.9 us
  Pallas kernels: 0 us -> 48.3 us
  starting transfers between devices: 32.8 us -> 74.8 us
  waiting for transfers between devices: 127 us -> 156 us
  matrix products: 21.8 us -> 0 us
  other arithmetic: 20.1 us -> 10.2 us
    ppermute x4 -> x12, waiting for transfers between devices: 0.01 us -> 48.7 us  [ring4(): second = lax.ppermute(from_next[h:], ax, bwd)]
    pallas_call x0 -> x2, Pallas kernels: none -> 48.3 us  [the longest x1 27.6 us: first_call(): pl.pallas_call(first_kernel, grid_spec=grid, out_shape=[jax.ShapeDtypeStr...]
    gather x3 -> x0, local copies, waits for them, and re-layouts: 29.5 us -> none  [the longest x1 10.6 us: body(): moved = jnp.take(psi_tiles, local_ids, axis=0)]
    ppermute x4 -> x12, waiting for transfers between devices: 37.4 us -> 9.83 us  [ring4(): from_prev = lax.ppermute(x, ax, fwd)]
    dot_general x1 -> x0, matrix products: 21.8 us -> none  [body(): jnp.einsum('kij,kjl->kil', chosen, half, preferred_element_type=jnp.float32)]
    ppermute x3 -> x4, waiting for transfers between devices: 89.6 us -> 68.3 us  [the longest x1 68.3 us: body(): remote = lax.ppermute(partial, 'xh', SWAP)]
    ppermute x4 -> x12, waiting for transfers between devices: 0.01 us -> 19.1 us  [ring4(): first = lax.ppermute(from_prev[:h], ax, fwd)]
    ppermute x4 -> x12, starting transfers between devices: 7.66 us -> 25.6 us  [ring4(): from_next = lax.ppermute(x, ax, bwd)]
  transfers between devices with their start and end apart: 19 -> 52, of which waited for: 5 -> 17; matrix products, arithmetic and copies ran while one was open for 19% -> 9% of each run, Pallas kernels for 0% -> 15%
where the time goes in v2:
time: 319 us; the launch traced here: 317 us
  waiting for transfers between devices  156 us (49%)
  starting transfers between devices  74.8 us (23%)
  Pallas kernels  48.3 us (15%)
  local copies, waits for them, and re-layouts  26.9 us (8%)
  other arithmetic  10.2 us (3%)
    ppermute x1, waiting for transfers between devices, body(): remote = lax.ppermute(partial, 'xh', SWAP)  68.3 us
    ppermute x12, waiting for transfers between devices, ring4(): second = lax.ppermute(from_next[h:], ax, bwd)  48.7 us
    pallas_call x1, Pallas kernels, first_call(): pl.pallas_call(first_kernel, grid_spec=grid, out_shape=[jax.ShapeDtypeStr...  27.6 us
    ppermute x12, starting transfers between devices, ring4(): from_next = lax.ppermute(x, ax, bwd)  25.6 us
    pallas_call x1, Pallas kernels, second_call(): pl.pallas_call(second_kernel, grid_spec=grid, out_shape=jax.ShapeDtypeStr...  20.7 us
    ppermute x12, starting transfers between devices, ring4(): second = lax.ppermute(from_next[h:], ax, bwd)  20.2 us
    ppermute x12, waiting for transfers between devices, ring4(): first = lax.ppermute(from_prev[:h], ax, fwd)  19.1 us
    ppermute x1, starting transfers between devices, body(): from_sib = lax.ppermute(to_sib, 'core', SWAP)  11.6 us
  transfers between devices with their start and end apart: 52, of which 17 were waited for; matrix products, arithmetic and copies ran while one was open for 9% of the time, Pallas kernels for 15%

profile of v2, /device:TPU:1, one launch (start us, length us, event | category | flops | bytes accessed | tf_op | source)
XLA Modules:
  0.0 317.1 jit_solution(8797844175508761470)
XLA Ops:
  0.0 3.6 %collective-permute-start = (bf16[16,16,512]{2,1,0:T(8,128)(2,1)}, bf16[16,16,512]{2,1,0:T(8,128)(2,1)S(1)}, u32[]{:S(2)}, u32[]{:S(2)}) collective-permute-start(bf16[16,16,512]{2,1,0:T(8,128)(2,1)} %bitcast.152), channel_id=1, source_target_pairs={{0,3},{1,0},{2,1},{3,2},{4,7},{5,4},{6,5},{7,6},{8,11},{9,8},{10,9... | collective-permute-start | bytes 786440 | tf_op jit(solution)/shard_map/ppermute | solution.py:17
  9.7 2.7 collective-permute-start.3
  14.4 3.2 collective-permute-done.2
  20.3 3.8 %collective-permute-start.25 = (bf16[16,16,256]{2,1,0:T(8,128)(2,1)S(1)}, bf16[16,16,256]{2,1,0:T(8,128)(2,1)S(1)}, u32[]{:S(2)}, u32[]{:S(2)}) collective-permute-start(bf16[16,16,256]{2,1,0:T(8,128)(2,1)S(1)} %get-tuple-element.15), channel_id=1, source_target_pairs={{0,12},{4,0},{8,4},{12,8},{1,13},{5,1},{9,5},{13,9},{2,14},{6,2},{... | collective-permute-start | bytes 393224 | tf_op jit(solution)/shard_map/ppermute | solution.py:17
  24.3 2.5 collective-permute-start.33
  27.0 2.7 collective-permute-start.41
  29.9 2.7 collective-permute-start.20
  33.3 2.7 collective-permute-start.4
  37.2 2.7 collective-permute-start.9
  42.3 18.6 %collective-permute-done.28 = bf16[8,16,256]{2,1,0:T(8,128)(2,1)S(1)} collective-permute-done((bf16[8,16,256]{2,1,0:T(8,128)(2,1)S(1)}, bf16[8,16,256]{2,1,0:T(8,128)(2,1)S(1)}, u32[]{:S(2)}, u32[]{:S(2)}) %collective-permute-start.28) | collective-permute-done | bytes 65568 | tf_op jit(solution)/shard_map/ppermute | solution.py:20
  68.2 5.9 %collective-permute-done.12 = bf16[8,16,512]{2,1,0:T(8,128)(2,1)S(1)} collective-permute-done((bf16[8,16,512]{2,1,0:T(8,128)(2,1)S(1)}, bf16[8,16,512]{2,1,0:T(8,128)(2,1)S(1)}, u32[]{:S(2)}, u32[]{:S(2)}) %collective-permute-start.12) | collective-permute-done | bytes 131104 | tf_op jit(solution)/shard_map/ppermute | solution.py:20
  75.0 2.4 collective-permute-start.29
  78.4 7.9 %collective-permute-done.22 = bf16[4,16,16,256]{3,2,1,0:T(8,128)(2,1)S(1)} collective-permute-done((bf16[4,16,16,256]{3,2,1,0:T(8,128)(2,1)S(1)}, bf16[4,16,16,256]{3,2,1,0:T(8,128)(2,1)S(1)}, u32[]{:S(2)}, u32[]{:S(2)}) %collective-permute-start.22) | collective-permute-done | bytes 524320 | tf_op jit(solution)/shard_map/ppermute | solution.py:16
  90.2 2.7 collective-permute-start.32
  93.1 3.3 %collective-permute-done.23 = bf16[2,16,16,256]{3,2,1,0:T(8,128)(2,1)S(1)} collective-permute-done((bf16[2,16,16,256]{3,2,1,0:T(8,128)(2,1)S(1)}, bf16[2,16,16,256]{3,2,1,0:T(8,128)(2,1)S(1)}, u32[]{:S(2)}, u32[]{:S(2)}) %collective-permute-start.23) | collective-permute-done | bytes 262176 | tf_op jit(solution)/shard_map/ppermute | solution.py:19
  96.4 2.7 collective-permute-start.36
  99.1 15.0 %collective-permute-done.32 = bf16[2,16,16,256]{3,2,1,0:T(8,128)(2,1)S(1)} collective-permute-done((bf16[2,16,16,256]{3,2,1,0:T(8,128)(2,1)S(1)}, bf16[2,16,16,256]{3,2,1,0:T(8,128)(2,1)S(1)}, u32[]{:S(2)}, u32[]{:S(2)}) %collective-permute-start.32) | collective-permute-done | bytes 262176 | tf_op jit(solution)/shard_map/ppermute | solution.py:20
  114.1 2.6 collective-permute-done.31
  119.8 2.7 collective-permute-done.7
  122.4 2.6 collective-permute-start.16
  126.5 4.7 %collective-permute-done.16 = bf16[2,16,16,512]{3,2,1,0:T(8,128)(2,1)S(1)} collective-permute-done((bf16[2,16,16,512]{3,2,1,0:T(8,128)(2,1)S(1)}, bf16[2,16,16,512]{3,2,1,0:T(8,128)(2,1)S(1)}, u32[]{:S(2)}, u32[]{:S(2)}) %collective-permute-start.16) | collective-permute-done | bytes 524320 | tf_op jit(solution)/shard_map/ppermute | solution.py:20
  131.7 4.7 %collective-permute-done.15 = bf16[2,16,16,512]{3,2,1,0:T(8,128)(2,1)S(1)} collective-permute-done((bf16[2,16,16,512]{3,2,1,0:T(8,128)(2,1)S(1)}, bf16[2,16,16,512]{3,2,1,0:T(8,128)(2,1)S(1)}, u32[]{:S(2)}, u32[]{:S(2)}) %collective-permute-start.15) | collective-permute-done | bytes 524320 | tf_op jit(solution)/shard_map/ppermute | solution.py:19
  138.7 27.6 %shard_map.55 = (bf16[24,512,512]{2,1,0:T(8,128)(2,1)}, bf16[24,256,512]{2,1,0:T(8,128)(2,1)}) custom-call(s32[24]{0:T(128)} %subtract_bitcast_fusion.src, s32[24]{0:T(128)} %get-tuple-element.18.s0, s32[24]{0:T(128)} %get-tuple-element.17.s1, s32[1]{0:T(128)} %bitcast.3.xl, bf16[24,512,512]{2,1,0:T(8,128)(2,1)} %psi_other.1, ...), custom_call_target="tpu_custom_call" | custom-call | flops 9663676416 | bytes 50331648 | tf_op jit(solution)/shard_map/pallas_call | solution.py:85
  166.2 3.9 %constant_dynamic-slice_fusion = bf16[24,128,512]{2,1,0:T(8,128)(2,1)} fusion(bf16[24,256,512]{2,1,0:T(8,128)(2,1)} %get-tuple-element.8, s32[]{:T(128)S(6)} %select_n.227), kind=kLoop, calls=%fused_computation.65 | loop fusion | bytes 6291460 | tf_op jit(solution)/shard_map/dynamic_slice | solution.py:142
  170.1 11.6 %collective-permute-start.50 = (bf16[24,128,512]{2,1,0:T(8,128)(2,1)}, bf16[24,128,512]{2,1,0:T(8,128)(2,1)}, u32[]{:S(2)}, u32[]{:S(2)}) collective-permute-start(bf16[24,128,512]{2,1,0:T(8,128)(2,1)} %constant_dynamic-slice_fusion), channel_id=1, source_target_pairs={{0,32},{32,0},{1,33},{33,1},{2,34},{34,2},{3,35},{35,3},{4,36},{36... | collective-permute-start | bytes 9437192 | tf_op jit(solution)/shard_map/ppermute | solution.py:143
  185.4 10.0 %collective-permute-done.37 = bf16[4,16,16,256]{3,2,1,0:T(8,128)(2,1)} collective-permute-done((bf16[4,16,16,256]{3,2,1,0:T(8,128)(2,1)S(1)}, bf16[4,16,16,256]{3,2,1,0:T(8,128)(2,1)}, u32[]{:S(2)}, u32[]{:S(2)}) %collective-permute-start.37) | collective-permute-done | bytes 524320 | tf_op jit(solution)/shard_map/ppermute | solution.py:17
  213.2 20.7 %shard_map.56 = bf16[24,256,512]{2,1,0:T(8,128)(2,1)} custom-call(s32[24]{0:T(128)} %get-tuple-element.18.s0, bf16[24,512,512]{2,1,0:T(8,128)(2,1)} %get-tuple-element.7.half_ref, bf16[4,4,16,16,256]{4,3,2,1,0:T(8,128)(2,1)} %copy-done.3, bf16[4,4,16,16,256]{4,3,2,1,0:T(8,128)(2,1)} %copy-done.2), custom_call_target="tpu_custom_call" | custom-call | flops 3221225472 | bytes 25165824 | tf_op jit(solution)/shard_map/pallas_call | solution.py:111
  236.3 2.4 collective-permute-start.49
  238.7 3.9 %add_convert_fusion.1 = bf16[24,128,512]{2,1,0:T(8,128)(2,1)S(1)} fusion(bf16[24,128,512]{2,1,0:T(8,128)(2,1)} %collective-permute-done.50, bf16[24,256,512]{2,1,0:T(8,128)(2,1)} %get-tuple-element.8, s32[]{:T(128)S(6)} %select_n.226), kind=kLoop, calls=%fused_computation.1 | loop fusion | flops 6291456 | bytes 9437188 | tf_op jit(solution)/shard_map/convert_element_type | solution.py:144
  242.6 2.8 collective-permute-start.51
  245.4 68.3 %collective-permute-done.51 = bf16[24,128,512]{2,1,0:T(8,128)(2,1)S(1)} collective-permute-done((bf16[24,128,512]{2,1,0:T(8,128)(2,1)S(1)}, bf16[24,128,512]{2,1,0:T(8,128)(2,1)S(1)}, u32[]{:S(2)}, u32[]{:S(2)}) %collective-permute-start.51) | collective-permute-done | bytes 3145760 | tf_op jit(solution)/shard_map/ppermute | solution.py:145
  313.7 3.4 %add_convert_fusion = bf16[24,128,512]{2,1,0:T(8,128)(2,1)} fusion(bf16[24,128,512]{2,1,0:T(8,128)(2,1)S(1)} %collective-permute-done.51, bf16[24,128,512]{2,1,0:T(8,128)(2,1)S(1)} %collective-permute-done.49, bf16[24,256,512]{2,1,0:T(8,128)(2,1)S(1)} %bitcast.151, s32[]{:T(128)S(6)} %select_n.226), kind=kLoop, calls=%fused_computation | loop fusion | flops 9437184 | bytes 12582916 | tf_op jit(solution)/shard_map/convert_element_type | solution.py:153
  (186 shorter events, 59.3 us)
Async XLA Ops:
  0.0 9.7 %collective-permute-start = (bf16[16,16,512]{2,1,0:T(8,128)(2,1)}, bf16[16,16,512]{2,1,0:T(8,128)(2,1)S(1)}, u32[]{:S(2)}, u32[]{:S(2)}) collective-permute-start(bf16[16,16,512]{2,1,0:T(8,128)(2,1)} %bitcast.152), channel_id=1, source_target_pairs={{0,3},{1,0},{2,1},{3,2},{4,7},{5,4},{6,5},{7,6},{8,11},{9,8},{10,9... | collective-permute-start | bytes 786440 | tf_op jit(solution)/shard_map/ppermute | solution.py:17
  4.6 13.6 %collective-permute-start.8 = (bf16[2,16,16,512]{3,2,1,0:T(8,128)(2,1)S(1)}, bf16[2,16,16,512]{3,2,1,0:T(8,128)(2,1)S(1)}, u32[]{:S(2)}, u32[]{:S(2)}) collective-permute-start(bf16[2,16,16,512]{3,2,1,0:T(8,128)(2,1)S(1)} %pad_maximum_fusion), channel_id=1, source_target_pairs={{0,16},{16,0},{1,17},{17,1},{2,18},{18,2},{3,19},{19,3},{4,20},{20... | collective-permute-start | bytes 1572872 | tf_op jit(solution)/shard_map/ppermute | solution.py:128
  20.3 9.6 %collective-permute-start.25 = (bf16[16,16,256]{2,1,0:T(8,128)(2,1)S(1)}, bf16[16,16,256]{2,1,0:T(8,128)(2,1)S(1)}, u32[]{:S(2)}, u32[]{:S(2)}) collective-permute-start(bf16[16,16,256]{2,1,0:T(8,128)(2,1)S(1)} %get-tuple-element.15), channel_id=1, source_target_pairs={{0,12},{4,0},{8,4},{12,8},{1,13},{5,1},{9,5},{13,9},{2,14},{6,2},{... | collective-permute-start | bytes 393224 | tf_op jit(solution)/shard_map/ppermute | solution.py:17
  27.0 9.6 %collective-permute-start.41 = (bf16[16,16,256]{2,1,0:T(8,128)(2,1)S(1)}, bf16[16,16,256]{2,1,0:T(8,128)(2,1)S(1)}, u32[]{:S(2)}, u32[]{:S(2)}) collective-permute-start(bf16[16,16,256]{2,1,0:T(8,128)(2,1)S(1)} %get-tuple-element.13), channel_id=1, source_target_pairs={{0,12},{4,0},{8,4},{12,8},{1,13},{5,1},{9,5},{13,9},{2,14},{6,2},{... | collective-permute-start | bytes 393224 | tf_op jit(solution)/shard_map/ppermute | solution.py:17
  29.9 10.7 %collective-permute-start.20 = (bf16[8,16,256]{2,1,0:T(8,128)(2,1)S(1)}, bf16[8,16,256]{2,1,0:T(8,128)(2,1)S(1)}, u32[]{:S(2)}, u32[]{:S(2)}) collective-permute-start(bf16[8,16,256]{2,1,0:T(8,128)(2,1)S(1)} %slice.140), channel_id=1, source_target_pairs={{0,3},{1,0},{2,1},{3,2},{4,7},{5,4},{6,5},{7,6},{8,11},{9,8},{10,9... | collective-permute-start | bytes 196616 | tf_op jit(solution)/shard_map/ppermute | solution.py:20
  33.3 56.3 %collective-permute-start.4 = (bf16[4,16,16,512]{3,2,1,0:T(8,128)(2,1)S(1)}, bf16[4,16,16,512]{3,2,1,0:T(8,128)(2,1)S(1)}, u32[]{:S(2)}, u32[]{:S(2)}) collective-permute-start(bf16[4,16,16,512]{3,2,1,0:T(8,128)(2,1)S(1)} %bitcast_dynamic-update-slice_fusion.20), channel_id=1, source_target_pairs={{0,12},{4,0},{8,4},{12,8},{1,13},{5,1},{9,5},{13,9},{2,14},{6,2},{... | collective-permute-start | bytes 3145736 | tf_op jit(solution)/shard_map/ppermute | solution.py:17
  36.6 53.6 %collective-permute-start.5 = (bf16[4,16,16,512]{3,2,1,0:T(8,128)(2,1)S(1)}, bf16[4,16,16,512]{3,2,1,0:T(8,128)(2,1)S(1)}, u32[]{:S(2)}, u32[]{:S(2)}) collective-permute-start(bf16[4,16,16,512]{3,2,1,0:T(8,128)(2,1)S(1)} %bitcast_dynamic-update-slice_fusion.20), channel_id=1, source_target_pairs={{0,4},{4,8},{8,12},{12,0},{1,5},{5,9},{9,13},{13,1},{2,6},{6,10},{... | collective-permute-start | bytes 3145736 | tf_op jit(solution)/shard_map/ppermute | solution.py:16
  37.2 27.4 %collective-permute-start.9 = (bf16[16,16,512]{2,1,0:T(8,128)(2,1)S(1)}, bf16[16,16,512]{2,1,0:T(8,128)(2,1)S(1)}, u32[]{:S(2)}, u32[]{:S(2)}) collective-permute-start(bf16[16,16,512]{2,1,0:T(8,128)(2,1)S(1)} %get-tuple-element.11), channel_id=1, source_target_pairs={{0,12},{4,0},{8,4},{12,8},{1,13},{5,1},{9,5},{13,9},{2,14},{6,2},{... | collective-permute-start | bytes 786440 | tf_op jit(solution)/shard_map/ppermute | solution.py:17
  40.5 20.4 %collective-permute-start.28 = (bf16[8,16,256]{2,1,0:T(8,128)(2,1)S(1)}, bf16[8,16,256]{2,1,0:T(8,128)(2,1)S(1)}, u32[]{:S(2)}, u32[]{:S(2)}) collective-permute-start(bf16[8,16,256]{2,1,0:T(8,128)(2,1)S(1)} %slice.145), channel_id=1, source_target_pairs={{0,12},{4,0},{8,4},{12,8},{1,13},{5,1},{9,5},{13,9},{2,14},{6,2},{... | collective-permute-start | bytes 196616 | tf_op jit(solution)/shard_map/ppermute | solution.py:20
  40.5 21.9 %collective-permute-start.27 = (bf16[8,16,256]{2,1,0:T(8,128)(2,1)S(1)}, bf16[8,16,256]{2,1,0:T(8,128)(2,1)S(1)}, u32[]{:S(2)}, u32[]{:S(2)}) collective-permute-start(bf16[8,16,256]{2,1,0:T(8,128)(2,1)S(1)} %slice.144), channel_id=1, source_target_pairs={{0,4},{4,8},{8,12},{12,0},{1,5},{5,9},{9,13},{13,1},{2,6},{6,10},{... | collective-permute-start | bytes 196616 | tf_op jit(solution)/shard_map/ppermute | solution.py:19
  62.4 15.0 %collective-permute-start.21 = (bf16[4,16,16,256]{3,2,1,0:T(8,128)(2,1)S(1)}, bf16[4,16,16,256]{3,2,1,0:T(8,128)(2,1)S(1)}, u32[]{:S(2)}, u32[]{:S(2)}) collective-permute-start(bf16[4,16,16,256]{3,2,1,0:T(8,128)(2,1)S(1)} %bitcast_dynamic-update-slice_fusion.31), channel_id=1, source_target_pairs={{0,12},{4,0},{8,4},{12,8},{1,13},{5,1},{9,5},{13,9},{2,14},{6,2},{... | collective-permute-start | bytes 1572872 | tf_op jit(solution)/shard_map/ppermute | solution.py:17
  64.6 9.4 %collective-permute-start.12 = (bf16[8,16,512]{2,1,0:T(8,128)(2,1)S(1)}, bf16[8,16,512]{2,1,0:T(8,128)(2,1)S(1)}, u32[]{:S(2)}, u32[]{:S(2)}) collective-permute-start(bf16[8,16,512]{2,1,0:T(8,128)(2,1)S(1)} %slice.134), channel_id=1, source_target_pairs={{0,12},{4,0},{8,4},{12,8},{1,13},{5,1},{9,5},{13,9},{2,14},{6,2},{... | collective-permute-start | bytes 393224 | tf_op jit(solution)/shard_map/ppermute | solution.py:20
  74.1 12.2 %collective-permute-start.22 = (bf16[4,16,16,256]{3,2,1,0:T(8,128)(2,1)S(1)}, bf16[4,16,16,256]{3,2,1,0:T(8,128)(2,1)S(1)}, u32[]{:S(2)}, u32[]{:S(2)}) collective-permute-start(bf16[4,16,16,256]{3,2,1,0:T(8,128)(2,1)S(1)} %bitcast_dynamic-update-slice_fusion.31), channel_id=1, source_target_pairs={{0,4},{4,8},{8,12},{12,0},{1,5},{5,9},{9,13},{13,1},{2,6},{6,10},{... | collective-permute-start | bytes 1572872 | tf_op jit(solution)/shard_map/ppermute | solution.py:16
  75.0 12.5 %collective-permute-start.29 = (bf16[4,16,16,256]{3,2,1,0:T(8,128)(2,1)S(1)}, bf16[4,16,16,256]{3,2,1,0:T(8,128)(2,1)S(1)}, u32[]{:S(2)}, u32[]{:S(2)}) collective-permute-start(bf16[4,16,16,256]{3,2,1,0:T(8,128)(2,1)S(1)} %bitcast_dynamic-update-slice_fusion.28), channel_id=1, source_target_pairs={{0,3},{1,0},{2,1},{3,2},{4,7},{5,4},{6,5},{7,6},{8,11},{9,8},{10,9... | collective-permute-start | bytes 1572872 | tf_op jit(solution)/shard_map/ppermute | solution.py:17
  77.4 12.0 %collective-permute-start.30 = (bf16[4,16,16,256]{3,2,1,0:T(8,128)(2,1)S(1)}, bf16[4,16,16,256]{3,2,1,0:T(8,128)(2,1)S(1)}, u32[]{:S(2)}, u32[]{:S(2)}) collective-permute-start(bf16[4,16,16,256]{3,2,1,0:T(8,128)(2,1)S(1)} %bitcast_dynamic-update-slice_fusion.28), channel_id=1, source_target_pairs={{0,1},{1,2},{2,3},{3,0},{4,5},{5,6},{6,7},{7,4},{8,9},{9,10},{10,1... | collective-permute-start | bytes 1572872 | tf_op jit(solution)/shard_map/ppermute | solution.py:16
  87.5 29.9 %collective-permute-start.13 = (bf16[4,16,16,512]{3,2,1,0:T(8,128)(2,1)S(1)}, bf16[4,16,16,512]{3,2,1,0:T(8,128)(2,1)S(1)}, u32[]{:S(2)}, u32[]{:S(2)}) collective-permute-start(bf16[4,16,16,512]{3,2,1,0:T(8,128)(2,1)S(1)} %bitcast_dynamic-update-slice_fusion.18), channel_id=1, source_target_pairs={{0,3},{1,0},{2,1},{3,2},{4,7},{5,4},{6,5},{7,6},{8,11},{9,8},{10,9... | collective-permute-start | bytes 3145736 | tf_op jit(solution)/shard_map/ppermute | solution.py:17
  89.5 28.1 %collective-permute-start.14 = (bf16[4,16,16,512]{3,2,1,0:T(8,128)(2,1)S(1)}, bf16[4,16,16,512]{3,2,1,0:T(8,128)(2,1)S(1)}, u32[]{:S(2)}, u32[]{:S(2)}) collective-permute-start(bf16[4,16,16,512]{3,2,1,0:T(8,128)(2,1)S(1)} %bitcast_dynamic-update-slice_fusion.18), channel_id=1, source_target_pairs={{0,1},{1,2},{2,3},{3,0},{4,5},{5,6},{6,7},{7,4},{8,9},{9,10},{10,1... | collective-permute-start | bytes 3145736 | tf_op jit(solution)/shard_map/ppermute | solution.py:16
  90.2 23.9 %collective-permute-start.32 = (bf16[2,16,16,256]{3,2,1,0:T(8,128)(2,1)S(1)}, bf16[2,16,16,256]{3,2,1,0:T(8,128)(2,1)S(1)}, u32[]{:S(2)}, u32[]{:S(2)}) collective-permute-start(bf16[2,16,16,256]{3,2,1,0:T(8,128)(2,1)S(1)} %slice.147), channel_id=1, source_target_pairs={{0,3},{1,0},{2,1},{3,2},{4,7},{5,4},{6,5},{7,6},{8,11},{9,8},{10,9... | collective-permute-start | bytes 786440 | tf_op jit(solution)/shard_map/ppermute | solution.py:20
  92.9 23.8 %collective-permute-start.31 = (bf16[2,16,16,256]{3,2,1,0:T(8,128)(2,1)S(1)}, bf16[2,16,16,256]{3,2,1,0:T(8,128)(2,1)S(1)}, u32[]{:S(2)}, u32[]{:S(2)}) collective-permute-start(bf16[2,16,16,256]{3,2,1,0:T(8,128)(2,1)S(1)} %slice.146), channel_id=1, source_target_pairs={{0,1},{1,2},{2,3},{3,0},{4,5},{5,6},{6,7},{7,4},{8,9},{9,10},{10,1... | collective-permute-start | bytes 786440 | tf_op jit(solution)/shard_map/ppermute | solution.py:19
  96.4 85.3 %collective-permute-start.36 = (bf16[8,16,256]{2,1,0:T(8,128)(2,1)}, bf16[8,16,256]{2,1,0:T(8,128)(2,1)S(1)}, u32[]{:S(2)}, u32[]{:S(2)}) collective-permute-start(bf16[8,16,256]{2,1,0:T(8,128)(2,1)} %slice.150), channel_id=1, source_target_pairs={{0,3},{1,0},{2,1},{3,2},{4,7},{5,4},{6,5},{7,6},{8,11},{9,8},{10,9... | collective-permute-start | bytes 196616 | tf_op jit(solution)/shard_map/ppermute | solution.py:20
  116.7 9.4 %collective-permute-start.6 = (bf16[2,16,16,512]{3,2,1,0:T(8,128)(2,1)S(1)}, bf16[2,16,16,512]{3,2,1,0:T(8,128)(2,1)S(1)}, u32[]{:S(2)}, u32[]{:S(2)}) collective-permute-start(bf16[2,16,16,512]{3,2,1,0:T(8,128)(2,1)S(1)} %slice.130), channel_id=1, source_target_pairs={{0,4},{4,8},{8,12},{12,0},{1,5},{5,9},{9,13},{13,1},{2,6},{6,10},{... | collective-permute-start | bytes 1572872 | tf_op jit(solution)/shard_map/ppermute | solution.py:19
  117.4 64.4 %collective-permute-start.35 = (bf16[8,16,256]{2,1,0:T(8,128)(2,1)}, bf16[8,16,256]{2,1,0:T(8,128)(2,1)S(1)}, u32[]{:S(2)}, u32[]{:S(2)}) collective-permute-start(bf16[8,16,256]{2,1,0:T(8,128)(2,1)} %slice.149), channel_id=1, source_target_pairs={{0,1},{1,2},{2,3},{3,0},{4,5},{5,6},{6,7},{7,4},{8,9},{9,10},{10,1... | collective-permute-start | bytes 196616 | tf_op jit(solution)/shard_map/ppermute | solution.py:19
  117.5 65.8 %collective-permute-start.44 = (bf16[8,16,256]{2,1,0:T(8,128)(2,1)}, bf16[8,16,256]{2,1,0:T(8,128)(2,1)S(1)}, u32[]{:S(2)}, u32[]{:S(2)}) collective-permute-start(bf16[8,16,256]{2,1,0:T(8,128)(2,1)} %slice.155), channel_id=1, source_target_pairs={{0,12},{4,0},{8,4},{12,8},{1,13},{5,1},{9,5},{13,9},{2,14},{6,2},{... | collective-permute-start | bytes 196616 | tf_op jit(solution)/shard_map/ppermute | solution.py:20
  126.1 10.2 %collective-permute-start.15 = (bf16[2,16,16,512]{3,2,1,0:T(8,128)(2,1)S(1)}, bf16[2,16,16,512]{3,2,1,0:T(8,128)(2,1)S(1)}, u32[]{:S(2)}, u32[]{:S(2)}) collective-permute-start(bf16[2,16,16,512]{3,2,1,0:T(8,128)(2,1)S(1)} %slice.135), channel_id=1, source_target_pairs={{0,1},{1,2},{2,3},{3,0},{4,5},{5,6},{6,7},{7,4},{8,9},{9,10},{10,1... | collective-permute-start | bytes 1572872 | tf_op jit(solution)/shard_map/ppermute | solution.py:19
  131.1 52.2 %collective-permute-start.43 = (bf16[8,16,256]{2,1,0:T(8,128)(2,1)}, bf16[8,16,256]{2,1,0:T(8,128)(2,1)S(1)}, u32[]{:S(2)}, u32[]{:S(2)}) collective-permute-start(bf16[8,16,256]{2,1,0:T(8,128)(2,1)} %slice.154), channel_id=1, source_target_pairs={{0,4},{4,8},{8,12},{12,0},{1,5},{5,9},{9,13},{13,1},{2,6},{6,10},{... | collective-permute-start | bytes 196616 | tf_op jit(solution)/shard_map/ppermute | solution.py:19
  170.1 68.6 %collective-permute-start.50 = (bf16[24,128,512]{2,1,0:T(8,128)(2,1)}, bf16[24,128,512]{2,1,0:T(8,128)(2,1)}, u32[]{:S(2)}, u32[]{:S(2)}) collective-permute-start(bf16[24,128,512]{2,1,0:T(8,128)(2,1)} %constant_dynamic-slice_fusion), channel_id=1, source_target_pairs={{0,32},{32,0},{1,33},{33,1},{2,34},{34,2},{3,35},{35,3},{4,36},{36... | collective-permute-start | bytes 9437192 | tf_op jit(solution)/shard_map/ppermute | solution.py:143
  181.8 13.7 %collective-permute-start.37 = (bf16[4,16,16,256]{3,2,1,0:T(8,128)(2,1)S(1)}, bf16[4,16,16,256]{3,2,1,0:T(8,128)(2,1)}, u32[]{:S(2)}, u32[]{:S(2)}) collective-permute-start(bf16[4,16,16,256]{3,2,1,0:T(8,128)(2,1)S(1)} %bitcast_dynamic-update-slice_fusion.25), channel_id=1, source_target_pairs={{0,12},{4,0},{8,4},{12,8},{1,13},{5,1},{9,5},{13,9},{2,14},{6,2},{... | collective-permute-start | bytes 1572872 | tf_op jit(solution)/shard_map/ppermute | solution.py:17
  181.9 16.1 %collective-permute-start.38 = (bf16[4,16,16,256]{3,2,1,0:T(8,128)(2,1)S(1)}, bf16[4,16,16,256]{3,2,1,0:T(8,128)(2,1)}, u32[]{:S(2)}, u32[]{:S(2)}) collective-permute-start(bf16[4,16,16,256]{3,2,1,0:T(8,128)(2,1)S(1)} %bitcast_dynamic-update-slice_fusion.25), channel_id=1, source_target_pairs={{0,4},{4,8},{8,12},{12,0},{1,5},{5,9},{9,13},{13,1},{2,6},{6,10},{... | collective-permute-start | bytes 1572872 | tf_op jit(solution)/shard_map/ppermute | solution.py:16
  183.4 15.7 %collective-permute-start.45 = (bf16[4,16,16,256]{3,2,1,0:T(8,128)(2,1)S(1)}, bf16[4,16,16,256]{3,2,1,0:T(8,128)(2,1)}, u32[]{:S(2)}, u32[]{:S(2)}) collective-permute-start(bf16[4,16,16,256]{3,2,1,0:T(8,128)(2,1)S(1)} %bitcast_dynamic-update-slice_fusion.22), channel_id=1, source_target_pairs={{0,3},{1,0},{2,1},{3,2},{4,7},{5,4},{6,5},{7,6},{8,11},{9,8},{10,9... | collective-permute-start | bytes 1572872 | tf_op jit(solution)/shard_map/ppermute | solution.py:17
  183.5 16.9 %collective-permute-start.46 = (bf16[4,16,16,256]{3,2,1,0:T(8,128)(2,1)S(1)}, bf16[4,16,16,256]{3,2,1,0:T(8,128)(2,1)}, u32[]{:S(2)}, u32[]{:S(2)}) collective-permute-start(bf16[4,16,16,256]{3,2,1,0:T(8,128)(2,1)S(1)} %bitcast_dynamic-update-slice_fusion.22), channel_id=1, source_target_pairs={{0,1},{1,2},{2,3},{3,0},{4,5},{5,6},{6,7},{7,4},{8,9},{9,10},{10,1... | collective-permute-start | bytes 1572872 | tf_op jit(solution)/shard_map/ppermute | solution.py:16
  236.3 9.1 %collective-permute-start.49 = (bf16[24,128,512]{2,1,0:T(8,128)(2,1)S(1)}, bf16[24,128,512]{2,1,0:T(8,128)(2,1)S(1)}, u32[]{:S(2)}, u32[]{:S(2)}) collective-permute-start(bf16[24,128,512]{2,1,0:T(8,128)(2,1)S(1)} %constant_dynamic-slice_fusion.1), channel_id=1, source_target_pairs={{0,32},{32,0},{1,33},{33,1},{2,34},{34,2},{3,35},{35,3},{4,36},{36... | collective-permute-start | bytes 9437192 | tf_op jit(solution)/shard_map/ppermute | solution.py:151
  242.6 71.1 %collective-permute-start.51 = (bf16[24,128,512]{2,1,0:T(8,128)(2,1)S(1)}, bf16[24,128,512]{2,1,0:T(8,128)(2,1)S(1)}, u32[]{:S(2)}, u32[]{:S(2)}) collective-permute-start(bf16[24,128,512]{2,1,0:T(8,128)(2,1)S(1)} %add_convert_fusion.1), channel_id=1, source_target_pairs={{0,64},{64,0},{1,65},{65,1},{2,66},{66,2},{3,67},{67,3},{4,68},{68... | collective-permute-start | bytes 9437192 | tf_op jit(solution)/shard_map/ppermute | solution.py:145
  (29 other events, 337.3 us)

commit v3 on v2

v3 whole, which is shorter than its diff:
```python
import jax
import jax.numpy as jnp
from jax import lax
from jax.experimental import pallas as pl
from jax.experimental.pallas import tpu as pltpu
from jax.sharding import Mesh, PartitionSpec as P

SEC = ("xl", "z", "y")
TERM = ("xh", "core")
PLANE = ("z", "y")
SWAP = [(0, 1), (1, 0)]


def ring4(x, ax, at):
    fwd = [(i, (i + 1) % 4) for i in range(4)]
    bwd = [(i, (i - 1) % 4) for i in range(4)]
    from_prev = lax.ppermute(x, ax, fwd)
    from_next = lax.ppermute(x, ax, bwd)
    h = x.shape[0] // 2
    first = lax.ppermute(from_prev[:h], ax, fwd)
    second = lax.ppermute(from_next[h:], ax, bwd)
    me = lax.axis_index(ax)
    rel = [x, from_next, jnp.concatenate([first, second]), from_prev]
    shape = x.shape[:at] + (4,) + x.shape[at:]
    buf = jnp.zeros(shape, x.dtype)
    for k in range(4):
        start = [0] * len(shape)
        start[at] = (me + k) % 4
        buf = lax.dynamic_update_slice(buf, jnp.expand_dims(rel[k], at), start)
    return buf


def first_kernel(src, s0, s1, xl, psi, ra, rb, la, lb, half_ref, out_ref):
    p = psi[...]
    cut = la.shape[-1]
    ra_v = ra[...].reshape(-1, cut)
    rb_v = rb[...].reshape(-1, cut)
    half_a = jnp.dot(p, ra_v, preferred_element_type=jnp.float32).astype(jnp.bfloat16)
    half_b = jnp.dot(p, rb_v, preferred_element_type=jnp.float32).astype(jnp.bfloat16)
    half_ref[:, :cut] = half_a
    half_ref[:, cut:] = half_b
    la_v = la[...].reshape(-1, cut)
    lb_v = lb[...].reshape(-1, cut)
    out_a = jnp.dot(la_v, half_a[:cut], preferred_element_type=jnp.float32)
    out_a += jnp.dot(lb_v, half_a[cut:], preferred_element_type=jnp.float32)
    out_b = jnp.dot(la_v, half_b[:cut], preferred_element_type=jnp.float32)
    out_b += jnp.dot(lb_v, half_b[cut:], preferred_element_type=jnp.float32)
    out_ref[:, :cut] = out_a.astype(out_ref.dtype)
    out_ref[:, cut:] = out_b.astype(out_ref.dtype)


def second_kernel(half_ref, l_ref, out_ref):
    out_ref[...] = jnp.dot(l_ref[...], half_ref[...], preferred_element_type=jnp.float32).astype(out_ref.dtype)


def first_call(src, s0, s1, xl, psi, ring_part, sc_part):
    tiles, width, _ = psi.shape
    cut = width // 2
    zr, yr = ring_part.shape[2], ring_part.shape[3]
    grid = pltpu.PrefetchScalarGridSpec(
        num_scalar_prefetch=4,
        grid=(tiles,),
        in_specs=[
            pl.BlockSpec((None, width, width), lambda k, src, s0, s1, xl: (src[k], 0, 0)),
            pl.BlockSpec((2, None, zr, yr, ring_part.shape[4], cut), lambda k, src, s0, s1, xl: (0, s1[k], 0, 0, 0, 0)),
            pl.BlockSpec((2, None, sc_part.shape[2], cut), lambda k, src, s0, s1, xl: (0, s1[k], 0, 0)),
            pl.BlockSpec((None, None, zr, yr, ring_part.shape[4], cut), lambda k, src, s0, s1, xl: (2, s0[k], 0, 0, 0, 0)),
            pl.BlockSpec((None, None, sc_part.shape[2], cut), lambda k, src, s0, s1, xl: (2, s0[k], 0, 0)),
        ],
        out_specs=[
            pl.BlockSpec((None, width, width), lambda k, src, s0, s1, xl: (k, 0, 0)),
            pl.BlockSpec((None, cut, width), lambda k, src, s0, s1, xl: (k, 0, 0)),
        ],
    )
    flops = tiles * (2 * width**3 + 2 * cut * width * width)
    return pl.pallas_call(
        first_kernel,
        grid_spec=grid,
        out_shape=[
            jax.ShapeDtypeStruct((tiles, width, width), jnp.bfloat16),
            jax.ShapeDtypeStruct((tiles, cut, width), jnp.bfloat16),
        ],
        compiler_params=pltpu.CompilerParams(dimension_semantics=("arbitrary",)),
        cost_estimate=pl.CostEstimate(flops=flops, transcendentals=0, bytes_accessed=tiles * width * width * 2 * 4),
    )(src, s0, s1, xl, psi, ring_part, sc_part, ring_part, sc_part)


def second_call(s0, half, l_late):
    tiles, width, _ = half.shape
    cut = width // 2
    grid = pltpu.PrefetchScalarGridSpec(
        num_scalar_prefetch=1,
        grid=(tiles,),
        in_specs=[
            pl.BlockSpec((None, width, width), lambda k, s0: (k, 0, 0)),
            pl.BlockSpec((None, cut, width), lambda k, s0: (s0[k], 0, 0)),
        ],
        out_specs=pl.BlockSpec((None, cut, width), lambda k, s0: (k, 0, 0)),
    )
    return pl.pallas_call(
        lambda s0, h, l, o: second_kernel(h, l, o),
        grid_spec=grid,
        out_shape=jax.ShapeDtypeStruct((tiles, cut, width), jnp.bfloat16),
        compiler_params=pltpu.CompilerParams(dimension_semantics=("arbitrary",)),
        cost_estimate=pl.CostEstimate(flops=tiles * 2 * cut * width * width, transcendentals=0, bytes_accessed=tiles * width * width * 2 * 2),
    )(s0, half, l_late)


def step(psi_tiles, sectors, sources, left_env, right_env):
    tile_count, width, _ = psi_tiles.shape
    cut = width // 2
    xh = lax.axis_index("xh")
    core = lax.axis_index("core")
    xl = lax.axis_index("xl")
    left, right = left_env[0], right_env[0]
    pair = lax.ppermute(jnp.stack([left, right]), "xl", SWAP)
    left_other, right_other = pair[0], pair[1]
    low = xl == 0
    r0 = jnp.where(low, right, right_other)
    r1 = jnp.where(low, right_other, right)
    own_is_early = xl != xh
    l_early = jnp.where(own_is_early, left, left_other)
    l_late = jnp.where(own_is_early, left_other, left)
    early = jnp.stack([r0, r1, l_early])
    ring_part = ring4(ring4(early[..., :cut], "y", 2), "z", 2)
    sc_part = lax.all_gather(early[..., cut:], PLANE, axis=2, tiled=True)
    late = lax.all_gather(l_late, PLANE, axis=1, tiled=True)
    src = (sources[0] - lax.axis_index(SEC) * tile_count).astype(jnp.int32)
    s0 = sectors[:, 0].astype(jnp.int32)
    s1 = sectors[:, 1].astype(jnp.int32)
    half, out_rem = first_call(src, s0, s1, xl.reshape(1).astype(jnp.int32), psi_tiles, ring_part, sc_part)
    rows = width // 4
    mine_rem = lax.dynamic_slice_in_dim(out_rem, core * rows, rows, 1)
    to_sib = lax.dynamic_slice_in_dim(out_rem, (1 - core) * rows, rows, 1)
    from_sib = lax.ppermute(to_sib, "core", SWAP)
    partial = (mine_rem.astype(jnp.float32) + from_sib.astype(jnp.float32)).astype(jnp.bfloat16)
    remote = lax.ppermute(partial, "xh", SWAP)
    out_loc = second_call(s0, half, late)
    mine_loc = lax.dynamic_slice_in_dim(out_loc, core * rows, rows, 1)
    to_sib2 = lax.dynamic_slice_in_dim(out_loc, (1 - core) * rows, rows, 1)
    from_sib2 = lax.ppermute(to_sib2, "core", SWAP)
    total = mine_loc.astype(jnp.float32) + from_sib2.astype(jnp.float32) + remote.astype(jnp.float32)
    return total.astype(jnp.bfloat16)


def solution(mesh):
    fine = Mesh(mesh.devices.reshape(2, 2, 2, 4, 4), TERM + SEC)
    placed = (
        P(SEC, None, None),
        P(SEC, None),
        P(TERM, SEC),
        P(TERM, None, SEC, None),
        P(TERM, None, SEC, None),
    )
    return jax.shard_map(step, mesh=fine, in_specs=placed, out_specs=P(SEC, TERM, None), check_vma=False)
```

time: 319 us -> 287 us (0.90)
  starting transfers between devices: 74.8 us -> 21.3 us
  waiting for transfers between devices: 156 us -> 174 us
  between operations: 1.03 us -> 13.6 us
  local copies, waits for them, and re-layouts: 26.9 us -> 16.2 us
    ppermute x12 -> x2, waiting for transfers between devices: 10.1 us -> 55.3 us  [ring4(): from_next = lax.ppermute(x, ax, bwd)]
    ppermute x12 -> x2, waiting for transfers between devices: 48.7 us -> 7.29 us  [ring4(): second = lax.ppermute(from_next[h:], ax, bwd)]
    ppermute x12 -> x2, starting transfers between devices: 25.6 us -> 5.82 us  [ring4(): from_next = lax.ppermute(x, ax, bwd)]
    ppermute x12 -> x2, starting transfers between devices: 20.2 us -> 5.09 us  [ring4(): second = lax.ppermute(from_next[h:], ax, bwd)]
    ppermute x4, waiting for transfers between devices: 68.3 us -> 79.6 us  [the longest x1 68.4 us: step(): remote = lax.ppermute(partial, 'xh', SWAP)]
    ppermute x12 -> x2, waiting for transfers between devices: 9.83 us -> 0.93 us  [ring4(): from_prev = lax.ppermute(x, ax, fwd)]
    all_gather x0 -> x2, waiting for transfers between devices: none -> 8.69 us  [the longest x1 8.69 us: step(): late = lax.all_gather(l_late, PLANE, axis=1, tiled=True)]
    ppermute x4, starting transfers between devices: 18.1 us -> 10.1 us  [the longest x1 4.31 us: step(): from_sib = lax.ppermute(to_sib, 'core', SWAP)]
  transfers between devices with their start and end apart: 52 -> 14, of which waited for: 17 -> 9; matrix products, arithmetic and copies ran while one was open for 9% -> 7% of each run, Pallas kernels for 15% -> 17%
where the time goes in v3:
time: 287 us; the launch traced here: 286 us
  waiting for transfers between devices  174 us (61%)
  Pallas kernels  48.7 us (17%)
  starting transfers between devices  21.3 us (7%)
  local copies, waits for them, and re-layouts  16.2 us (6%)
  between operations  13.6 us (5%)
  other arithmetic  12.2 us (4%)
    ppermute x1, waiting for transfers between devices, step(): remote = lax.ppermute(partial, 'xh', SWAP)  68.4 us
    ppermute x2, waiting for transfers between devices, ring4(): from_next = lax.ppermute(x, ax, bwd)  55.3 us
    pallas_call x1, Pallas kernels, first_call(): pl.pallas_call(first_kernel, grid_spec=grid, out_shape=[jax.ShapeDtypeStr...  28 us
    ppermute x2, waiting for transfers between devices, ring4(): first = lax.ppermute(from_prev[:h], ax, fwd)  21.8 us
    pallas_call x1, Pallas kernels, second_call(): pl.pallas_call(lambda s0, h, l, o: second_kernel(h, l, o), grid_spec=grid...  20.7 us
    ppermute x1, waiting for transfers between devices, step(): pair = lax.ppermute(jnp.stack([left, right]), 'xl', SWAP)  11.2 us
    all_gather x1, waiting for transfers between devices, step(): late = lax.all_gather(l_late, PLANE, axis=1, tiled=True)  8.69 us
    ppermute x2, waiting for transfers between devices, ring4(): second = lax.ppermute(from_next[h:], ax, bwd)  7.29 us
  transfers between devices with their start and end apart: 14, of which 9 were waited for; matrix products, arithmetic and copies ran while one was open for 7% of the time, Pallas kernels for 17%

profile of v3, /device:TPU:1, one launch (start us, length us, event | category | flops | bytes accessed | tf_op | source)
XLA Modules:
  0.0 285.7 jit_solution(1503250252781761615)
XLA Ops:
  6.5 1.1 pad_maximum_fusion.1
  7.6 2.1 collective-permute-start
  9.7 11.2 %collective-permute-done = bf16[2,16,16,512]{3,2,1,0:T(8,128)(2,1)S(1)} collective-permute-done((bf16[2,16,16,512]{3,2,1,0:T(8,128)(2,1)S(1)}, bf16[2,16,16,512]{3,2,1,0:T(8,128)(2,1)S(1)}, u32[]{:S(2)}, u32[]{:S(2)}) %collective-permute-start) | collective-permute-done | bytes 524320 | tf_op jit(solution)/shard_map/ppermute | solution.py:116
  20.9 1.8 broadcast_select_fusion
  22.9 0.8 fusion.2
  23.7 3.2 %collective-permute-start.1 = (bf16[3,16,16,256]{3,2,1,0:T(8,128)(2,1)S(1)}, bf16[3,16,16,256]{3,2,1,0:T(8,128)(2,1)S(1)}, u32[]{:S(2)}, u32[]{:S(2)}) collective-permute-start(bf16[3,16,16,256]{3,2,1,0:T(8,128)(2,1)S(1)} %get-tuple-element.12), channel_id=1, source_target_pairs={{0,3},{1,0},{2,1},{3,2},{4,7},{5,4},{6,5},{7,6},{8,11},{9,8},{10,9... | collective-permute-start | bytes 1179656 | tf_op jit(solution)/shard_map/ppermute | solution.py:18
  27.1 6.8 %collective-permute-done.1 = bf16[3,16,16,256]{3,2,1,0:T(8,128)(2,1)S(1)} collective-permute-done((bf16[3,16,16,256]{3,2,1,0:T(8,128)(2,1)S(1)}, bf16[3,16,16,256]{3,2,1,0:T(8,128)(2,1)S(1)}, u32[]{:S(2)}, u32[]{:S(2)}) %collective-permute-start.1) | collective-permute-done | bytes 393248 | tf_op jit(solution)/shard_map/ppermute | solution.py:18
  33.9 3.5 %collective-permute-start.4 = (bf16[2,16,16,256]{3,2,1,0:T(8,128)(2,1)S(1)}, bf16[2,16,16,256]{3,2,1,0:T(8,128)(2,1)S(1)}, u32[]{:S(2)}, u32[]{:S(2)}) collective-permute-start(bf16[2,16,16,256]{3,2,1,0:T(8,128)(2,1)S(1)} %slice.44), channel_id=1, source_target_pairs={{0,3},{1,0},{2,1},{3,2},{4,7},{5,4},{6,5},{7,6},{8,11},{9,8},{10,9... | collective-permute-start | bytes 786440 | tf_op jit(solution)/shard_map/ppermute | solution.py:21
  37.8 7.7 %collective-permute-done.3 = bf16[1,16,16,256]{3,2,1,0:T(8,128)(2,1)S(1)} collective-permute-done((bf16[1,16,16,256]{3,2,1,0:T(8,128)(2,1)S(1)}, bf16[1,16,16,256]{3,2,1,0:T(8,128)(2,1)S(1)}, u32[]{:S(2)}, u32[]{:S(2)}) %collective-permute-start.3) | collective-permute-done | bytes 131104 | tf_op jit(solution)/shard_map/ppermute | solution.py:20
  45.6 2.6 collective-permute-start.5
  48.2 48.6 %collective-permute-done.5 = bf16[3,16,4,16,256]{4,3,2,1,0:T(8,128)(2,1)S(1)} collective-permute-done((bf16[3,16,4,16,256]{4,3,2,1,0:T(8,128)(2,1)S(1)}, bf16[3,16,4,16,256]{4,3,2,1,0:T(8,128)(2,1)S(1)}, u32[]{:S(2)}, u32[]{:S(2)}) %collective-permute-start.5) | collective-permute-done | bytes 1572896 | tf_op jit(solution)/shard_map/ppermute | solution.py:18
  96.9 1.6 collective-permute-start.8
  99.6 0.9 collective-permute-done.6
  100.5 1.1 slice.45
  101.7 3.5 %broadcast_in_dim.30 = bf16[3,16,4,4,16,256]{5,4,3,2,1,0:T(8,128)(2,1)} broadcast(bf16[]{:T(256)} %constant.70.clone.1), dimensions={} | broadcast | bytes 6291458 | tf_op jit(solution)/shard_map/broadcast_in_dim | solution.py:25
  105.2 1.2 bitcast_dynamic-update-slice_fusion.1
  106.4 1.3 bitcast_dynamic-update-slice_fusion
  107.7 14.2 %collective-permute-done.7 = bf16[1,16,4,16,256]{4,3,2,1,0:T(8,128)(2,1)S(1)} collective-permute-done((bf16[1,16,4,16,256]{4,3,2,1,0:T(8,128)(2,1)S(1)}, bf16[1,16,4,16,256]{4,3,2,1,0:T(8,128)(2,1)S(1)}, u32[]{:S(2)}, u32[]{:S(2)}) %collective-permute-start.7) | collective-permute-done | bytes 524320 | tf_op jit(solution)/shard_map/ppermute | solution.py:20
  121.8 7.3 %collective-permute-done.8 = bf16[2,16,4,16,256]{4,3,2,1,0:T(8,128)(2,1)S(1)} collective-permute-done((bf16[2,16,4,16,256]{4,3,2,1,0:T(8,128)(2,1)S(1)}, bf16[2,16,4,16,256]{4,3,2,1,0:T(8,128)(2,1)S(1)}, u32[]{:S(2)}, u32[]{:S(2)}) %collective-permute-start.8) | collective-permute-done | bytes 1048608 | tf_op jit(solution)/shard_map/ppermute | solution.py:21
  129.1 1.3 fusion
  130.5 2.7 bitcast_dynamic-update-slice_fusion.2.ra.la
  133.2 28.0 %shard_map.55 = (bf16[24,512,512]{2,1,0:T(8,128)(2,1)}, bf16[24,256,512]{2,1,0:T(8,128)(2,1)}) custom-call(s32[24]{0:T(128)} %subtract_bitcast_fusion.src, s32[24]{0:T(128)} %get-tuple-element.18.s0, s32[24]{0:T(128)} %get-tuple-element.17.s1, s32[1]{0:T(128)} %bitcast.3.xl, bf16[24,512,512]{2,1,0:T(8,128)(2,1)} %psi.1, ...), custom_call_target="tpu_custom_call" | custom-call | flops 9663676416 | bytes 50331648 | tf_op jit(solution)/shard_map/pallas_call | solution.py:76
  161.2 2.2 constant_dynamic-slice_fusion
  163.4 4.3 %collective-permute-start.10 = (bf16[24,128,512]{2,1,0:T(8,128)(2,1)S(1)}, bf16[24,128,512]{2,1,0:T(8,128)(2,1)}, u32[]{:S(2)}, u32[]{:S(2)}) collective-permute-start(bf16[24,128,512]{2,1,0:T(8,128)(2,1)S(1)} %constant_dynamic-slice_fusion), channel_id=1, source_target_pairs={{0,32},{32,0},{1,33},{33,1},{2,34},{34,2},{3,35},{35,3},{4,36},{36... | collective-permute-start | bytes 9437192 | tf_op jit(solution)/shard_map/ppermute | solution.py:135
  167.7 8.7 %all-gather.6.cloned.1.call-done = bf16[1,16,256,512]{3,2,1,0:T(8,128)(2,1)} async-done(((bf16[1,16,16,512]{3,2,1,0:T(8,128)(2,1)}), bf16[1,16,256,512]{3,2,1,0:T(8,128)(2,1)}) %all-gather.6.cloned.1.call-update) | async-done | bytes 4194320 | tf_op jit(solution)/shard_map/all_gather | solution.py:127
  176.4 20.7 %shard_map.56 = bf16[24,256,512]{2,1,0:T(8,128)(2,1)} custom-call(s32[24]{0:T(128)} %get-tuple-element.18.s0, bf16[24,512,512]{2,1,0:T(8,128)(2,1)} %get-tuple-element.7.h, bf16[16,256,512]{2,1,0:T(8,128)(2,1)} %bitcast.44), custom_call_target="tpu_custom_call" | custom-call | flops 3221225472 | bytes 25165824 | tf_op jit(solution)/shard_map/pallas_call | solution.py:100
  197.1 2.4 constant_dynamic-slice_fusion.1
  199.5 1.0 collective-permute-start.9
  200.4 3.9 %add_convert_fusion.1 = bf16[24,128,512]{2,1,0:T(8,128)(2,1)S(1)} fusion(bf16[24,128,512]{2,1,0:T(8,128)(2,1)} %collective-permute-done.10, bf16[24,256,512]{2,1,0:T(8,128)(2,1)} %get-tuple-element.8, s32[]{:T(128)S(6)} %select_n.118), kind=kLoop, calls=%fused_computation.1 | loop fusion | flops 6291456 | bytes 9437188 | tf_op jit(solution)/shard_map/convert_element_type | solution.py:136
  204.4 2.7 collective-permute-start.11
  207.1 68.4 %collective-permute-done.11 = bf16[24,128,512]{2,1,0:T(8,128)(2,1)S(1)} collective-permute-done((bf16[24,128,512]{2,1,0:T(8,128)(2,1)S(1)}, bf16[24,128,512]{2,1,0:T(8,128)(2,1)S(1)}, u32[]{:S(2)}, u32[]{:S(2)}) %collective-permute-start.11) | collective-permute-done | bytes 3145760 | tf_op jit(solution)/shard_map/ppermute | solution.py:137
  275.5 3.4 %add_convert_fusion = bf16[24,128,512]{2,1,0:T(8,128)(2,1)} fusion(bf16[24,128,512]{2,1,0:T(8,128)(2,1)S(1)} %collective-permute-done.11, bf16[24,128,512]{2,1,0:T(8,128)(2,1)S(1)} %collective-permute-done.9, bf16[24,256,512]{2,1,0:T(8,128)(2,1)S(1)} %bitcast.43, s32[]{:T(128)S(6)} %select_n.118), kind=kLoop, calls=%fused_computation | loop fusion | flops 9437184 | bytes 12582916 | tf_op jit(solution)/shard_map/convert_element_type | solution.py:143
  (33 shorter events, 2.0 us)
Async XLA Ops:
  6.5 126.7 %all-gather.4.cloned.1.call-start = ((), (), s32[]{:S(2)}) async-start(), calls=%async_computation | async-start | bytes 6684672 | tf_op jit(solution)/shard_map/all_gather | solution.py:126
  7.6 13.3 %collective-permute-start = (bf16[2,16,16,512]{3,2,1,0:T(8,128)(2,1)S(1)}, bf16[2,16,16,512]{3,2,1,0:T(8,128)(2,1)S(1)}, u32[]{:S(2)}, u32[]{:S(2)}) collective-permute-start(bf16[2,16,16,512]{3,2,1,0:T(8,128)(2,1)S(1)} %pad_maximum_fusion.1), channel_id=1, source_target_pairs={{0,16},{16,0},{1,17},{17,1},{2,18},{18,2},{3,19},{19,3},{4,20},{20... | collective-permute-start | bytes 1572872 | tf_op jit(solution)/shard_map/ppermute | solution.py:116
  23.7 152.7 %all-gather.6.cloned.1.call-start = ((), (), s32[]{:S(2)}) async-start(), calls=%async_computation.1 | async-start | bytes 4456448 | tf_op jit(solution)/shard_map/all_gather | solution.py:127
  23.7 10.1 %collective-permute-start.1 = (bf16[3,16,16,256]{3,2,1,0:T(8,128)(2,1)S(1)}, bf16[3,16,16,256]{3,2,1,0:T(8,128)(2,1)S(1)}, u32[]{:S(2)}, u32[]{:S(2)}) collective-permute-start(bf16[3,16,16,256]{3,2,1,0:T(8,128)(2,1)S(1)} %get-tuple-element.12), channel_id=1, source_target_pairs={{0,3},{1,0},{2,1},{3,2},{4,7},{5,4},{6,5},{7,6},{8,11},{9,8},{10,9... | collective-permute-start | bytes 1179656 | tf_op jit(solution)/shard_map/ppermute | solution.py:18
  27.0 10.7 %collective-permute-start.2 = (bf16[3,16,16,256]{3,2,1,0:T(8,128)(2,1)S(1)}, bf16[3,16,16,256]{3,2,1,0:T(8,128)(2,1)S(1)}, u32[]{:S(2)}, u32[]{:S(2)}) collective-permute-start(bf16[3,16,16,256]{3,2,1,0:T(8,128)(2,1)S(1)} %get-tuple-element.12), channel_id=1, source_target_pairs={{0,1},{1,2},{2,3},{3,0},{4,5},{5,6},{6,7},{7,4},{8,9},{9,10},{10,1... | collective-permute-start | bytes 1179656 | tf_op jit(solution)/shard_map/ppermute | solution.py:17
  33.9 11.6 %collective-permute-start.4 = (bf16[2,16,16,256]{3,2,1,0:T(8,128)(2,1)S(1)}, bf16[2,16,16,256]{3,2,1,0:T(8,128)(2,1)S(1)}, u32[]{:S(2)}, u32[]{:S(2)}) collective-permute-start(bf16[2,16,16,256]{3,2,1,0:T(8,128)(2,1)S(1)} %slice.44), channel_id=1, source_target_pairs={{0,3},{1,0},{2,1},{3,2},{4,7},{5,4},{6,5},{7,6},{8,11},{9,8},{10,9... | collective-permute-start | bytes 786440 | tf_op jit(solution)/shard_map/ppermute | solution.py:21
  37.6 60.9 %copy-start.1 = (s32[1,24]{1,0:T(1,128)S(1)}, s32[1,24]{1,0:T(1,128)}, u32[]{:S(2)}) copy-start(s32[1,24]{1,0:T(1,128)} %param.7) | copy-start | bytes 292
  37.6 61.4 %copy-start = (s32[24,2]{0,1:T(2,128)S(1)}, s32[24,2]{0,1:T(2,128)}, u32[]{:S(2)}) copy-start(s32[24,2]{0,1:T(2,128)} %param.6) | copy-start | bytes 580
  37.7 7.8 %collective-permute-start.3 = (bf16[1,16,16,256]{3,2,1,0:T(8,128)(2,1)S(1)}, bf16[1,16,16,256]{3,2,1,0:T(8,128)(2,1)S(1)}, u32[]{:S(2)}, u32[]{:S(2)}) collective-permute-start(bf16[1,16,16,256]{3,2,1,0:T(8,128)(2,1)S(1)} %slice.43), channel_id=1, source_target_pairs={{0,1},{1,2},{2,3},{3,0},{4,5},{5,6},{6,7},{7,4},{8,9},{9,10},{10,1... | collective-permute-start | bytes 393224 | tf_op jit(solution)/shard_map/ppermute | solution.py:20
  45.6 51.2 %collective-permute-start.5 = (bf16[3,16,4,16,256]{4,3,2,1,0:T(8,128)(2,1)S(1)}, bf16[3,16,4,16,256]{4,3,2,1,0:T(8,128)(2,1)S(1)}, u32[]{:S(2)}, u32[]{:S(2)}) collective-permute-start(bf16[3,16,4,16,256]{4,3,2,1,0:T(8,128)(2,1)S(1)} %bitcast_dynamic-update-slice_fusion.3), channel_id=1, source_target_pairs={{0,12},{4,0},{8,4},{12,8},{1,13},{5,1},{9,5},{13,9},{2,14},{6,2},{... | collective-permute-start | bytes 4718600 | tf_op jit(solution)/shard_map/ppermute | solution.py:18
  48.2 52.3 %collective-permute-start.6 = (bf16[3,16,4,16,256]{4,3,2,1,0:T(8,128)(2,1)S(1)}, bf16[3,16,4,16,256]{4,3,2,1,0:T(8,128)(2,1)}, u32[]{:S(2)}, u32[]{:S(2)}) collective-permute-start(bf16[3,16,4,16,256]{4,3,2,1,0:T(8,128)(2,1)S(1)} %bitcast_dynamic-update-slice_fusion.3), channel_id=1, source_target_pairs={{0,4},{4,8},{8,12},{12,0},{1,5},{5,9},{9,13},{13,1},{2,6},{6,10},{... | collective-permute-start | bytes 4718600 | tf_op jit(solution)/shard_map/ppermute | solution.py:17
  96.9 32.3 %collective-permute-start.8 = (bf16[2,16,4,16,256]{4,3,2,1,0:T(8,128)(2,1)S(1)}, bf16[2,16,4,16,256]{4,3,2,1,0:T(8,128)(2,1)S(1)}, u32[]{:S(2)}, u32[]{:S(2)}) collective-permute-start(bf16[2,16,4,16,256]{4,3,2,1,0:T(8,128)(2,1)S(1)} %slice.46), channel_id=1, source_target_pairs={{0,12},{4,0},{8,4},{12,8},{1,13},{5,1},{9,5},{13,9},{2,14},{6,2},{... | collective-permute-start | bytes 3145736 | tf_op jit(solution)/shard_map/ppermute | solution.py:21
  101.6 20.2 %collective-permute-start.7 = (bf16[1,16,4,16,256]{4,3,2,1,0:T(8,128)(2,1)S(1)}, bf16[1,16,4,16,256]{4,3,2,1,0:T(8,128)(2,1)S(1)}, u32[]{:S(2)}, u32[]{:S(2)}) collective-permute-start(bf16[1,16,4,16,256]{4,3,2,1,0:T(8,128)(2,1)S(1)} %slice.45), channel_id=1, source_target_pairs={{0,4},{4,8},{8,12},{12,0},{1,5},{5,9},{9,13},{13,1},{2,6},{6,10},{... | collective-permute-start | bytes 1572872 | tf_op jit(solution)/shard_map/ppermute | solution.py:20
  163.4 37.0 %collective-permute-start.10 = (bf16[24,128,512]{2,1,0:T(8,128)(2,1)S(1)}, bf16[24,128,512]{2,1,0:T(8,128)(2,1)}, u32[]{:S(2)}, u32[]{:S(2)}) collective-permute-start(bf16[24,128,512]{2,1,0:T(8,128)(2,1)S(1)} %constant_dynamic-slice_fusion), channel_id=1, source_target_pairs={{0,32},{32,0},{1,33},{33,1},{2,34},{34,2},{3,35},{35,3},{4,36},{36... | collective-permute-start | bytes 9437192 | tf_op jit(solution)/shard_map/ppermute | solution.py:135
  197.1 78.4 %slice-start = ((s8[6291456]{0:T(1024)(128)(4,1)}), s8[4194304]{0:T(1024)(128)(4,1)S(1)}, s32[]{:S(2)}) async-start(s8[6291456]{0:T(1024)(128)(4,1)} %bitcast.42), calls=%async_computation.2 | async-start | bytes 8388608
  199.5 76.0 %slice-start.1 = ((s8[6291456]{0:T(1024)(128)(4,1)}), s8[2097152]{0:T(1024)(128)(4,1)S(1)}, s32[]{:S(2)}) async-start(s8[6291456]{0:T(1024)(128)(4,1)} %bitcast.42), calls=%async_computation.3 | async-start | bytes 4194304
  199.5 7.6 %collective-permute-start.9 = (bf16[24,128,512]{2,1,0:T(8,128)(2,1)S(1)}, bf16[24,128,512]{2,1,0:T(8,128)(2,1)S(1)}, u32[]{:S(2)}, u32[]{:S(2)}) collective-permute-start(bf16[24,128,512]{2,1,0:T(8,128)(2,1)S(1)} %constant_dynamic-slice_fusion.1), channel_id=1, source_target_pairs={{0,32},{32,0},{1,33},{33,1},{2,34},{34,2},{3,35},{35,3},{4,36},{36... | collective-permute-start | bytes 9437192 | tf_op jit(solution)/shard_map/ppermute | solution.py:141
  204.4 71.1 %collective-permute-start.11 = (bf16[24,128,512]{2,1,0:T(8,128)(2,1)S(1)}, bf16[24,128,512]{2,1,0:T(8,128)(2,1)S(1)}, u32[]{:S(2)}, u32[]{:S(2)}) collective-permute-start(bf16[24,128,512]{2,1,0:T(8,128)(2,1)S(1)} %add_convert_fusion.1), channel_id=1, source_target_pairs={{0,64},{64,0},{1,65},{65,1},{2,66},{66,2},{3,67},{67,3},{4,68},{68... | collective-permute-start | bytes 9437192 | tf_op jit(solution)/shard_map/ppermute | solution.py:137
Sparse Core Ops, SparseCore 0:
  23.8 97.0 all-gather.3
  123.1 53.2 all-gather.5

commit v4 on v3

--- a/solution.py
+++ b/solution.py
@@ -54,7 +54,7 @@
 
 
 def first_call(src, s0, s1, xl, psi, ring_part, sc_part):
-    tiles, width, _ = psi.shape
+    tiles, width = src.shape[0], psi.shape[1]
     cut = width // 2
     zr, yr = ring_part.shape[2], ring_part.shape[3]
     grid = pltpu.PrefetchScalarGridSpec(
@@ -128,19 +128,29 @@
     src = (sources[0] - lax.axis_index(SEC) * tile_count).astype(jnp.int32)
     s0 = sectors[:, 0].astype(jnp.int32)
     s1 = sectors[:, 1].astype(jnp.int32)
-    half, out_rem = first_call(src, s0, s1, xl.reshape(1).astype(jnp.int32), psi_tiles, ring_part, sc_part)
     rows = width // 4
-    mine_rem = lax.dynamic_slice_in_dim(out_rem, core * rows, rows, 1)
-    to_sib = lax.dynamic_slice_in_dim(out_rem, (1 - core) * rows, rows, 1)
-    from_sib = lax.ppermute(to_sib, "core", SWAP)
-    partial = (mine_rem.astype(jnp.float32) + from_sib.astype(jnp.float32)).astype(jnp.bfloat16)
-    remote = lax.ppermute(partial, "xh", SWAP)
-    out_loc = second_call(s0, half, late)
-    mine_loc = lax.dynamic_slice_in_dim(out_loc, core * rows, rows, 1)
-    to_sib2 = lax.dynamic_slice_in_dim(out_loc, (1 - core) * rows, rows, 1)
-    from_sib2 = lax.ppermute(to_sib2, "core", SWAP)
-    total = mine_loc.astype(jnp.float32) + from_sib2.astype(jnp.float32) + remote.astype(jnp.float32)
-    return total.astype(jnp.bfloat16)
+    chunks = 2
+    per = tile_count // chunks
+    xl_arg = xl.reshape(1).astype(jnp.int32)
+    results = []
+    pending = []
+    for part in range(chunks):
+        span = slice(part * per, (part + 1) * per)
+        half, out_rem = first_call(src[span], s0[span], s1[span], xl_arg, psi_tiles, ring_part, sc_part)
+        mine_rem = lax.dynamic_slice_in_dim(out_rem, core * rows, rows, 1)
+        to_sib = lax.dynamic_slice_in_dim(out_rem, (1 - core) * rows, rows, 1)
+        from_sib = lax.ppermute(to_sib, "core", SWAP)
+        partial = (mine_rem.astype(jnp.float32) + from_sib.astype(jnp.float32)).astype(jnp.bfloat16)
+        remote = lax.ppermute(partial, "xh", SWAP)
+        pending.append((span, half, remote))
+    for span, half, remote in pending:
+        out_loc = second_call(s0[span], half, late)
+        mine_loc = lax.dynamic_slice_in_dim(out_loc, core * rows, rows, 1)
+        to_sib2 = lax.dynamic_slice_in_dim(out_loc, (1 - core) * rows, rows, 1)
+        from_sib2 = lax.ppermute(to_sib2, "core", SWAP)
+        total = mine_loc.astype(jnp.float32) + from_sib2.astype(jnp.float32) + remote.astype(jnp.float32)
+        results.append(total.astype(jnp.bfloat16))
+    return jnp.concatenate(results, axis=0)
 
 
 def solution(mesh):

time: 287 us -> 287 us (level)
  waiting for transfers between devices: 174 us -> 163 us
  Pallas kernels: 48.7 us -> 53.4 us
  local copies, waits for them, and re-layouts: 16.2 us -> 20.6 us
    ppermute x1 -> x2, waiting for transfers between devices: 68.4 us -> 62.5 us  [step(): remote = lax.ppermute(partial, 'xh', SWAP)]
    all_gather x1, waiting for transfers between devices: 8.69 us -> 3.5 us  [step(): late = lax.all_gather(l_late, PLANE, axis=1, tiled=True)]
    dynamic_slice x1 -> x2, local copies, waits for them, and re-layouts: 2.21 us -> 5.31 us  [step(): to_sib = lax.dynamic_slice_in_dim(out_rem, (1 - core) * rows, rows, 1)]
    pallas_call x1 -> x2, Pallas kernels: 28 us -> 30.6 us  [first_call(): pl.pallas_call(first_kernel, grid_spec=grid, out_shape=[jax.ShapeDtypeStr...]
    pallas_call x1 -> x2, Pallas kernels: 20.7 us -> 22.8 us  [second_call(): pl.pallas_call(lambda s0, h, l, o: second_kernel(h, l, o), grid_spec=grid...]
  transfers between devices with their start and end apart: 14 -> 17, of which waited for: 9 -> 11; matrix products, arithmetic and copies ran while one was open for 7% -> 10% of each run, Pallas kernels for 17% -> 19%
where the time goes in v4:
time: 287 us; the launch traced here: 286 us
  waiting for transfers between devices  163 us (57%)
  Pallas kernels  53.4 us (19%)
  starting transfers between devices  22.1 us (8%)
  local copies, waits for them, and re-layouts  20.6 us (7%)
  between operations  13.6 us (5%)
  other arithmetic  13.3 us (5%)
    ppermute x2, waiting for transfers between devices, step(): remote = lax.ppermute(partial, 'xh', SWAP)  62.5 us
    ppermute x2, waiting for transfers between devices, ring4(): from_next = lax.ppermute(x, ax, bwd)  53.9 us
    pallas_call x2, Pallas kernels, first_call(): pl.pallas_call(first_kernel, grid_spec=grid, out_shape=[jax.ShapeDtypeStr...  30.6 us
    pallas_call x2, Pallas kernels, second_call(): pl.pallas_call(lambda s0, h, l, o: second_kernel(h, l, o), grid_spec=grid...  22.8 us
    ppermute x2, waiting for transfers between devices, ring4(): first = lax.ppermute(from_prev[:h], ax, fwd)  21.5 us
    ppermute x1, waiting for transfers between devices, step(): pair = lax.ppermute(jnp.stack([left, right]), 'xl', SWAP)  11.2 us
    ppermute x2, waiting for transfers between devices, ring4(): second = lax.ppermute(from_next[h:], ax, bwd)  8.7 us
    ppermute x2, starting transfers between devices, ring4(): from_next = lax.ppermute(x, ax, bwd)  5.81 us
  transfers between devices with their start and end apart: 17, of which 11 were waited for; matrix products, arithmetic and copies ran while one was open for 10% of the time, Pallas kernels for 19%

profile of v4, /device:TPU:1, one launch (start us, length us, event | category | flops | bytes accessed | tf_op | source)
XLA Modules:
  0.0 285.7 jit_solution(4675167411204188778)
XLA Ops:
  7.6 2.1 collective-permute-start
  9.7 11.2 %collective-permute-done = bf16[2,16,16,512]{3,2,1,0:T(8,128)(2,1)S(1)} collective-permute-done((bf16[2,16,16,512]{3,2,1,0:T(8,128)(2,1)S(1)}, bf16[2,16,16,512]{3,2,1,0:T(8,128)(2,1)S(1)}, u32[]{:S(2)}, u32[]{:S(2)}) %collective-permute-start) | collective-permute-done | bytes 524320 | tf_op jit(solution)/shard_map/ppermute | solution.py:116
  20.9 1.8 broadcast_select_fusion
  24.4 3.2 %collective-permute-start.1 = (bf16[3,16,16,256]{3,2,1,0:T(8,128)(2,1)S(1)}, bf16[3,16,16,256]{3,2,1,0:T(8,128)(2,1)S(1)}, u32[]{:S(2)}, u32[]{:S(2)}) collective-permute-start(bf16[3,16,16,256]{3,2,1,0:T(8,128)(2,1)S(1)} %get-tuple-element.16), channel_id=1, source_target_pairs={{0,3},{1,0},{2,1},{3,2},{4,7},{5,4},{6,5},{7,6},{8,11},{9,8},{10,9... | collective-permute-start | bytes 1179656 | tf_op jit(solution)/shard_map/ppermute | solution.py:18
  27.6 6.9 %collective-permute-done.1 = bf16[3,16,16,256]{3,2,1,0:T(8,128)(2,1)S(1)} collective-permute-done((bf16[3,16,16,256]{3,2,1,0:T(8,128)(2,1)S(1)}, bf16[3,16,16,256]{3,2,1,0:T(8,128)(2,1)S(1)}, u32[]{:S(2)}, u32[]{:S(2)}) %collective-permute-start.1) | collective-permute-done | bytes 393248 | tf_op jit(solution)/shard_map/ppermute | solution.py:18
  34.6 3.5 %collective-permute-start.4 = (bf16[2,16,16,256]{3,2,1,0:T(8,128)(2,1)S(1)}, bf16[2,16,16,256]{3,2,1,0:T(8,128)(2,1)S(1)}, u32[]{:S(2)}, u32[]{:S(2)}) collective-permute-start(bf16[2,16,16,256]{3,2,1,0:T(8,128)(2,1)S(1)} %slice.92), channel_id=1, source_target_pairs={{0,3},{1,0},{2,1},{3,2},{4,7},{5,4},{6,5},{7,6},{8,11},{9,8},{10,9... | collective-permute-start | bytes 786440 | tf_op jit(solution)/shard_map/ppermute | solution.py:21
  38.5 6.4 %collective-permute-done.3 = bf16[1,16,16,256]{3,2,1,0:T(8,128)(2,1)S(1)} collective-permute-done((bf16[1,16,16,256]{3,2,1,0:T(8,128)(2,1)S(1)}, bf16[1,16,16,256]{3,2,1,0:T(8,128)(2,1)S(1)}, u32[]{:S(2)}, u32[]{:S(2)}) %collective-permute-start.3) | collective-permute-done | bytes 131104 | tf_op jit(solution)/shard_map/ppermute | solution.py:20
  45.1 2.6 collective-permute-start.5
  47.7 46.9 %collective-permute-done.5 = bf16[3,16,4,16,256]{4,3,2,1,0:T(8,128)(2,1)S(1)} collective-permute-done((bf16[3,16,4,16,256]{4,3,2,1,0:T(8,128)(2,1)S(1)}, bf16[3,16,4,16,256]{4,3,2,1,0:T(8,128)(2,1)S(1)}, u32[]{:S(2)}, u32[]{:S(2)}) %collective-permute-start.5) | collective-permute-done | bytes 1572896 | tf_op jit(solution)/shard_map/ppermute | solution.py:18
  98.6 3.4 %broadcast_in_dim.30 = bf16[3,16,4,4,16,256]{5,4,3,2,1,0:T(8,128)(2,1)} broadcast(bf16[]{:T(256)} %constant.70.clone.1), dimensions={} | broadcast | bytes 6291458 | tf_op jit(solution)/shard_map/broadcast_in_dim | solution.py:25
  102.0 1.3 bitcast_dynamic-update-slice_fusion.1
  103.4 1.3 bitcast_dynamic-update-slice_fusion
  104.7 15.1 %collective-permute-done.7 = bf16[1,16,4,16,256]{4,3,2,1,0:T(8,128)(2,1)S(1)} collective-permute-done((bf16[1,16,4,16,256]{4,3,2,1,0:T(8,128)(2,1)S(1)}, bf16[1,16,4,16,256]{4,3,2,1,0:T(8,128)(2,1)S(1)}, u32[]{:S(2)}, u32[]{:S(2)}) %collective-permute-start.7) | collective-permute-done | bytes 524320 | tf_op jit(solution)/shard_map/ppermute | solution.py:20
  119.8 8.7 %collective-permute-done.8 = bf16[2,16,4,16,256]{4,3,2,1,0:T(8,128)(2,1)S(1)} collective-permute-done((bf16[2,16,4,16,256]{4,3,2,1,0:T(8,128)(2,1)S(1)}, bf16[2,16,4,16,256]{4,3,2,1,0:T(8,128)(2,1)S(1)}, u32[]{:S(2)}, u32[]{:S(2)}) %collective-permute-start.8) | collective-permute-done | bytes 1048608 | tf_op jit(solution)/shard_map/ppermute | solution.py:21
  128.4 1.4 fusion
  129.9 2.8 bitcast_dynamic-update-slice_fusion.2.ra.la
  132.7 15.1 %shard_map.55 = (bf16[12,512,512]{2,1,0:T(8,128)(2,1)}, bf16[12,256,512]{2,1,0:T(8,128)(2,1)}) custom-call(s32[12]{0:T(128)} %get-tuple-element.25.src, s32[12]{0:T(128)} %get-tuple-element.22.s0, s32[12]{0:T(128)} %get-tuple-element.21.s1, s32[1]{0:T(128)} %bitcast.3.xl, bf16[24,512,512]{2,1,0:T(8,128)(2,1)} %psi.3, ...), custom_call_target="tpu_custom_call" | custom-call | flops 4831838208 | bytes 25165824 | tf_op jit(solution)/shard_map/pallas_call | solution.py:76
  147.8 2.7 constant_dynamic-slice_fusion.2
  150.4 4.4 %collective-permute-start.10 = (bf16[12,128,512]{2,1,0:T(8,128)(2,1)}, bf16[12,128,512]{2,1,0:T(8,128)(2,1)}, u32[]{:S(2)}, u32[]{:S(2)}) collective-permute-start(bf16[12,128,512]{2,1,0:T(8,128)(2,1)} %constant_dynamic-slice_fusion.2), channel_id=1, source_target_pairs={{0,32},{32,0},{1,33},{33,1},{2,34},{34,2},{3,35},{35,3},{4,36},{36... | collective-permute-start | bytes 4718600 | tf_op jit(solution)/shard_map/ppermute | solution.py:142
  154.8 15.5 %shard_map.57 = (bf16[12,512,512]{2,1,0:T(8,128)(2,1)}, bf16[12,256,512]{2,1,0:T(8,128)(2,1)}) custom-call(s32[12]{0:T(128)} %get-tuple-element.26.src, s32[12]{0:T(128)} %get-tuple-element.24.s0, s32[12]{0:T(128)} %get-tuple-element.23.s1, s32[1]{0:T(128)} %bitcast.3.xl, bf16[24,512,512]{2,1,0:T(8,128)(2,1)} %psi.3, ...), custom_call_target="tpu_custom_call" | custom-call | flops 4831838208 | bytes 25165824 | tf_op jit(solution)/shard_map/pallas_call | solution.py:76
  170.3 2.7 constant_dynamic-slice_fusion
  173.0 3.5 %all-gather.6.cloned.1.call-done = bf16[1,16,256,512]{3,2,1,0:T(8,128)(2,1)} async-done(((bf16[1,16,16,512]{3,2,1,0:T(8,128)(2,1)}), bf16[1,16,256,512]{3,2,1,0:T(8,128)(2,1)}) %all-gather.6.cloned.1.call-update) | async-done | bytes 4194320 | tf_op jit(solution)/shard_map/all_gather | solution.py:127
  176.5 11.3 %shard_map.56 = bf16[12,256,512]{2,1,0:T(8,128)(2,1)} custom-call(s32[12]{0:T(128)} %get-tuple-element.22.s0, bf16[12,512,512]{2,1,0:T(8,128)(2,1)} %get-tuple-element.9.h, bf16[16,256,512]{2,1,0:T(8,128)(2,1)} %bitcast.48), custom_call_target="tpu_custom_call" | custom-call | flops 1610612736 | bytes 12582912 | tf_op jit(solution)/shard_map/pallas_call | solution.py:100
  187.8 2.7 constant_dynamic-slice_fusion.3
  191.4 11.5 %shard_map.58 = bf16[12,256,512]{2,1,0:T(8,128)(2,1)} custom-call(s32[12]{0:T(128)} %get-tuple-element.24.s0, bf16[12,512,512]{2,1,0:T(8,128)(2,1)} %get-tuple-element.11.h, bf16[16,256,512]{2,1,0:T(8,128)(2,1)} %bitcast.49), custom_call_target="tpu_custom_call" | custom-call | flops 1610612736 | bytes 12582912 | tf_op jit(solution)/shard_map/pallas_call | solution.py:100
  202.9 2.0 add_convert_fusion.3
  204.9 2.8 collective-permute-start.11
  208.3 2.1 add_convert_fusion.1
  211.6 30.9 %collective-permute-done.11 = bf16[12,128,512]{2,1,0:T(8,128)(2,1)S(1)} collective-permute-done((bf16[12,128,512]{2,1,0:T(8,128)(2,1)S(1)}, bf16[12,128,512]{2,1,0:T(8,128)(2,1)S(1)}, u32[]{:S(2)}, u32[]{:S(2)}) %collective-permute-start.11) | collective-permute-done | bytes 1572896 | tf_op jit(solution)/shard_map/ppermute | solution.py:144
  242.5 2.1 add_convert_fusion.2
  244.6 31.6 %collective-permute-done.14 = bf16[12,128,512]{2,1,0:T(8,128)(2,1)S(1)} collective-permute-done((bf16[12,128,512]{2,1,0:T(8,128)(2,1)S(1)}, bf16[12,128,512]{2,1,0:T(8,128)(2,1)S(1)}, u32[]{:S(2)}, u32[]{:S(2)}) %collective-permute-start.14) | collective-permute-done | bytes 1572896 | tf_op jit(solution)/shard_map/ppermute | solution.py:144
  276.9 1.9 pad_maximum_fusion
  (50 shorter events, 10.6 us)
Async XLA Ops:
  6.5 126.1 %all-gather.4.cloned.1.call-start = ((), (), s32[]{:S(2)}) async-start(), calls=%async_computation | async-start | bytes 6684672 | tf_op jit(solution)/shard_map/all_gather | solution.py:126
  7.6 13.3 %collective-permute-start = (bf16[2,16,16,512]{3,2,1,0:T(8,128)(2,1)S(1)}, bf16[2,16,16,512]{3,2,1,0:T(8,128)(2,1)S(1)}, u32[]{:S(2)}, u32[]{:S(2)}) collective-permute-start(bf16[2,16,16,512]{3,2,1,0:T(8,128)(2,1)S(1)} %pad_maximum_fusion.2), channel_id=1, source_target_pairs={{0,16},{16,0},{1,17},{17,1},{2,18},{18,2},{3,19},{19,3},{4,20},{20... | collective-permute-start | bytes 1572872 | tf_op jit(solution)/shard_map/ppermute | solution.py:116
  23.7 152.8 %all-gather.6.cloned.1.call-start = ((), (), s32[]{:S(2)}) async-start(), calls=%async_computation.1 | async-start | bytes 4456448 | tf_op jit(solution)/shard_map/all_gather | solution.py:127
  24.4 10.1 %collective-permute-start.1 = (bf16[3,16,16,256]{3,2,1,0:T(8,128)(2,1)S(1)}, bf16[3,16,16,256]{3,2,1,0:T(8,128)(2,1)S(1)}, u32[]{:S(2)}, u32[]{:S(2)}) collective-permute-start(bf16[3,16,16,256]{3,2,1,0:T(8,128)(2,1)S(1)} %get-tuple-element.16), channel_id=1, source_target_pairs={{0,3},{1,0},{2,1},{3,2},{4,7},{5,4},{6,5},{7,6},{8,11},{9,8},{10,9... | collective-permute-start | bytes 1179656 | tf_op jit(solution)/shard_map/ppermute | solution.py:18
  27.6 10.7 %collective-permute-start.2 = (bf16[3,16,16,256]{3,2,1,0:T(8,128)(2,1)S(1)}, bf16[3,16,16,256]{3,2,1,0:T(8,128)(2,1)S(1)}, u32[]{:S(2)}, u32[]{:S(2)}) collective-permute-start(bf16[3,16,16,256]{3,2,1,0:T(8,128)(2,1)S(1)} %get-tuple-element.16), channel_id=1, source_target_pairs={{0,1},{1,2},{2,3},{3,0},{4,5},{5,6},{6,7},{7,4},{8,9},{9,10},{10,1... | collective-permute-start | bytes 1179656 | tf_op jit(solution)/shard_map/ppermute | solution.py:17
  34.6 10.4 %collective-permute-start.4 = (bf16[2,16,16,256]{3,2,1,0:T(8,128)(2,1)S(1)}, bf16[2,16,16,256]{3,2,1,0:T(8,128)(2,1)S(1)}, u32[]{:S(2)}, u32[]{:S(2)}) collective-permute-start(bf16[2,16,16,256]{3,2,1,0:T(8,128)(2,1)S(1)} %slice.92), channel_id=1, source_target_pairs={{0,3},{1,0},{2,1},{3,2},{4,7},{5,4},{6,5},{7,6},{8,11},{9,8},{10,9... | collective-permute-start | bytes 786440 | tf_op jit(solution)/shard_map/ppermute | solution.py:21
  38.3 9.4 %copy-start.5 = (s32[1,24]{1,0:T(1,128)S(1)}, s32[1,24]{1,0:T(1,128)}, u32[]{:S(2)}) copy-start(s32[1,24]{1,0:T(1,128)} %param.7) | copy-start | bytes 292
  38.3 6.6 %collective-permute-start.3 = (bf16[1,16,16,256]{3,2,1,0:T(8,128)(2,1)S(1)}, bf16[1,16,16,256]{3,2,1,0:T(8,128)(2,1)S(1)}, u32[]{:S(2)}, u32[]{:S(2)}) collective-permute-start(bf16[1,16,16,256]{3,2,1,0:T(8,128)(2,1)S(1)} %slice.91), channel_id=1, source_target_pairs={{0,1},{1,2},{2,3},{3,0},{4,5},{5,6},{6,7},{7,4},{8,9},{9,10},{10,1... | collective-permute-start | bytes 393224 | tf_op jit(solution)/shard_map/ppermute | solution.py:20
  45.0 50.4 %copy-start.4 = (s32[24,2]{0,1:T(2,128)S(1)}, s32[24,2]{0,1:T(2,128)}, u32[]{:S(2)}) copy-start(s32[24,2]{0,1:T(2,128)} %param.6) | copy-start | bytes 580
  45.1 49.5 %collective-permute-start.5 = (bf16[3,16,4,16,256]{4,3,2,1,0:T(8,128)(2,1)S(1)}, bf16[3,16,4,16,256]{4,3,2,1,0:T(8,128)(2,1)S(1)}, u32[]{:S(2)}, u32[]{:S(2)}) collective-permute-start(bf16[3,16,4,16,256]{4,3,2,1,0:T(8,128)(2,1)S(1)} %bitcast_dynamic-update-slice_fusion.3), channel_id=1, source_target_pairs={{0,12},{4,0},{8,4},{12,8},{1,13},{5,1},{9,5},{13,9},{2,14},{6,2},{... | collective-permute-start | bytes 4718600 | tf_op jit(solution)/shard_map/ppermute | solution.py:18
  47.7 49.0 %collective-permute-start.6 = (bf16[3,16,4,16,256]{4,3,2,1,0:T(8,128)(2,1)S(1)}, bf16[3,16,4,16,256]{4,3,2,1,0:T(8,128)(2,1)}, u32[]{:S(2)}, u32[]{:S(2)}) collective-permute-start(bf16[3,16,4,16,256]{4,3,2,1,0:T(8,128)(2,1)S(1)} %bitcast_dynamic-update-slice_fusion.3), channel_id=1, source_target_pairs={{0,4},{4,8},{8,12},{12,0},{1,5},{5,9},{9,13},{13,1},{2,6},{6,10},{... | collective-permute-start | bytes 4718600 | tf_op jit(solution)/shard_map/ppermute | solution.py:17
  94.7 33.7 %collective-permute-start.8 = (bf16[2,16,4,16,256]{4,3,2,1,0:T(8,128)(2,1)S(1)}, bf16[2,16,4,16,256]{4,3,2,1,0:T(8,128)(2,1)S(1)}, u32[]{:S(2)}, u32[]{:S(2)}) collective-permute-start(bf16[2,16,4,16,256]{4,3,2,1,0:T(8,128)(2,1)S(1)} %slice.94), channel_id=1, source_target_pairs={{0,12},{4,0},{8,4},{12,8},{1,13},{5,1},{9,5},{13,9},{2,14},{6,2},{... | collective-permute-start | bytes 3145736 | tf_op jit(solution)/shard_map/ppermute | solution.py:21
  97.7 22.0 %collective-permute-start.7 = (bf16[1,16,4,16,256]{4,3,2,1,0:T(8,128)(2,1)S(1)}, bf16[1,16,4,16,256]{4,3,2,1,0:T(8,128)(2,1)S(1)}, u32[]{:S(2)}, u32[]{:S(2)}) collective-permute-start(bf16[1,16,4,16,256]{4,3,2,1,0:T(8,128)(2,1)S(1)} %slice.93), channel_id=1, source_target_pairs={{0,4},{4,8},{8,12},{12,0},{1,5},{5,9},{9,13},{13,1},{2,6},{6,10},{... | collective-permute-start | bytes 1572872 | tf_op jit(solution)/shard_map/ppermute | solution.py:20
  150.4 52.5 %collective-permute-start.10 = (bf16[12,128,512]{2,1,0:T(8,128)(2,1)}, bf16[12,128,512]{2,1,0:T(8,128)(2,1)}, u32[]{:S(2)}, u32[]{:S(2)}) collective-permute-start(bf16[12,128,512]{2,1,0:T(8,128)(2,1)} %constant_dynamic-slice_fusion.2), channel_id=1, source_target_pairs={{0,32},{32,0},{1,33},{33,1},{2,34},{34,2},{3,35},{35,3},{4,36},{36... | collective-permute-start | bytes 4718600 | tf_op jit(solution)/shard_map/ppermute | solution.py:142
  173.0 35.3 %collective-permute-start.13 = (bf16[12,128,512]{2,1,0:T(8,128)(2,1)}, bf16[12,128,512]{2,1,0:T(8,128)(2,1)}, u32[]{:S(2)}, u32[]{:S(2)}) collective-permute-start(bf16[12,128,512]{2,1,0:T(8,128)(2,1)} %constant_dynamic-slice_fusion), channel_id=1, source_target_pairs={{0,32},{32,0},{1,33},{33,1},{2,34},{34,2},{3,35},{35,3},{4,36},{36... | collective-permute-start | bytes 4718600 | tf_op jit(solution)/shard_map/ppermute | solution.py:142
  190.5 21.1 %collective-permute-start.9 = (bf16[12,128,512]{2,1,0:T(8,128)(2,1)}, bf16[12,128,512]{2,1,0:T(8,128)(2,1)}, u32[]{:S(2)}, u32[]{:S(2)}) collective-permute-start(bf16[12,128,512]{2,1,0:T(8,128)(2,1)} %constant_dynamic-slice_fusion.3), channel_id=1, source_target_pairs={{0,32},{32,0},{1,33},{33,1},{2,34},{34,2},{3,35},{35,3},{4,36},{36... | collective-permute-start | bytes 4718600 | tf_op jit(solution)/shard_map/ppermute | solution.py:150
  191.4 11.5 %copy-start.3 = (bf16[12,256,512]{2,1,0:T(8,128)(2,1)S(1)}, bf16[12,256,512]{2,1,0:T(8,128)(2,1)}, u32[]{:S(2)}) copy-start(bf16[12,256,512]{2,1,0:T(8,128)(2,1)} %get-tuple-element.10) | copy-start | bytes 9437188
  202.9 4.8 %copy-start = (bf16[12,256,512]{2,1,0:T(8,128)(2,1)S(1)}, bf16[12,256,512]{2,1,0:T(8,128)(2,1)}, u32[]{:S(2)}) copy-start(bf16[12,256,512]{2,1,0:T(8,128)(2,1)} %shard_map.58) | copy-start | bytes 9437188
  204.9 3.4 %copy-start.2 = (bf16[12,256,512]{2,1,0:T(8,128)(2,1)S(1)}, bf16[12,256,512]{2,1,0:T(8,128)(2,1)}, u32[]{:S(2)}) copy-start(bf16[12,256,512]{2,1,0:T(8,128)(2,1)} %get-tuple-element.12) | copy-start | bytes 9437188
  204.9 37.5 %collective-permute-start.11 = (bf16[12,128,512]{2,1,0:T(8,128)(2,1)S(1)}, bf16[12,128,512]{2,1,0:T(8,128)(2,1)S(1)}, u32[]{:S(2)}, u32[]{:S(2)}) collective-permute-start(bf16[12,128,512]{2,1,0:T(8,128)(2,1)S(1)} %add_convert_fusion.3), channel_id=1, source_target_pairs={{0,64},{64,0},{1,65},{65,1},{2,66},{66,2},{3,67},{67,3},{4,68},{68... | collective-permute-start | bytes 4718600 | tf_op jit(solution)/shard_map/ppermute | solution.py:144
  207.9 34.6 %copy-start.1 = (bf16[12,256,512]{2,1,0:T(8,128)(2,1)S(1)}, bf16[12,256,512]{2,1,0:T(8,128)(2,1)}, u32[]{:S(2)}) copy-start(bf16[12,256,512]{2,1,0:T(8,128)(2,1)} %shard_map.56) | copy-start | bytes 9437188
  207.9 36.7 %collective-permute-start.12 = (bf16[12,128,512]{2,1,0:T(8,128)(2,1)S(1)}, bf16[12,128,512]{2,1,0:T(8,128)(2,1)S(1)}, u32[]{:S(2)}, u32[]{:S(2)}) collective-permute-start(bf16[12,128,512]{2,1,0:T(8,128)(2,1)S(1)} %constant_dynamic-slice_fusion.1), channel_id=1, source_target_pairs={{0,32},{32,0},{1,33},{33,1},{2,34},{34,2},{3,35},{35,3},{4,36},{36... | collective-permute-start | bytes 4718600 | tf_op jit(solution)/shard_map/ppermute | solution.py:150
  210.4 65.8 %collective-permute-start.14 = (bf16[12,128,512]{2,1,0:T(8,128)(2,1)S(1)}, bf16[12,128,512]{2,1,0:T(8,128)(2,1)S(1)}, u32[]{:S(2)}, u32[]{:S(2)}) collective-permute-start(bf16[12,128,512]{2,1,0:T(8,128)(2,1)S(1)} %add_convert_fusion.1), channel_id=1, source_target_pairs={{0,64},{64,0},{1,65},{65,1},{2,66},{66,2},{3,67},{67,3},{4,68},{68... | collective-permute-start | bytes 4718600 | tf_op jit(solution)/shard_map/ppermute | solution.py:144
Sparse Core Ops, SparseCore 0:
  23.8 96.3 all-gather.3
  122.4 54.0 all-gather.5

commit v5 on v4

--- a/solution.py
+++ b/solution.py
@@ -63,9 +63,9 @@
         in_specs=[
             pl.BlockSpec((None, width, width), lambda k, src, s0, s1, xl: (src[k], 0, 0)),
             pl.BlockSpec((2, None, zr, yr, ring_part.shape[4], cut), lambda k, src, s0, s1, xl: (0, s1[k], 0, 0, 0, 0)),
-            pl.BlockSpec((2, None, sc_part.shape[2], cut), lambda k, src, s0, s1, xl: (0, s1[k], 0, 0)),
+            pl.BlockSpec((2, None, zr, yr, ring_part.shape[4], cut), lambda k, src, s0, s1, xl: (0, s1[k], 0, 0, 0, 0)),
             pl.BlockSpec((None, None, zr, yr, ring_part.shape[4], cut), lambda k, src, s0, s1, xl: (2, s0[k], 0, 0, 0, 0)),
-            pl.BlockSpec((None, None, sc_part.shape[2], cut), lambda k, src, s0, s1, xl: (2, s0[k], 0, 0)),
+            pl.BlockSpec((None, None, zr, yr, ring_part.shape[4], cut), lambda k, src, s0, s1, xl: (2, s0[k], 0, 0, 0, 0)),
         ],
         out_specs=[
             pl.BlockSpec((None, width, width), lambda k, src, s0, s1, xl: (k, 0, 0)),
@@ -123,7 +123,7 @@
     l_late = jnp.where(own_is_early, left_other, left)
     early = jnp.stack([r0, r1, l_early])
     ring_part = ring4(ring4(early[..., :cut], "y", 2), "z", 2)
-    sc_part = lax.all_gather(early[..., cut:], PLANE, axis=2, tiled=True)
+    sc_part = ring4(ring4(early[..., cut:], "z", 2), "y", 3)
     late = lax.all_gather(l_late, PLANE, axis=1, tiled=True)
     src = (sources[0] - lax.axis_index(SEC) * tile_count).astype(jnp.int32)
     s0 = sectors[:, 0].astype(jnp.int32)

time: 287 us -> 264 us (0.920)
  waiting for transfers between devices: 163 us -> 106 us
  local copies, waits for them, and re-layouts: 20.6 us -> 37.3 us
  starting transfers between devices: 22.1 us -> 35.3 us
  other arithmetic: 13.3 us -> 16.9 us
    ppermute x2, waiting for transfers between devices: 62.5 us -> 35.7 us  [step(): remote = lax.ppermute(partial, 'xh', SWAP)]
    ppermute x2 -> x4, waiting for transfers between devices: 21.5 us -> 8.1 us  [ring4(): first = lax.ppermute(from_prev[:h], ax, fwd)]
    ppermute x2 -> x4, starting transfers between devices: 3.6 us -> 12.3 us  [ring4(): second = lax.ppermute(from_next[h:], ax, bwd)]
    dynamic_update_slice x6 -> x12, local copies, waits for them, and re-layouts: 5.55 us -> 14 us  [ring4(): buf = lax.dynamic_update_slice(buf, jnp.expand_dims(rel[k], at), start)]
    another operation x0 -> x4, local copies, waits for them, and re-layouts: none -> 7.2 us
    ppermute x2 -> x4, waiting for transfers between devices: 8.7 us -> 1.82 us  [ring4(): second = lax.ppermute(from_next[h:], ax, bwd)]
    ppermute x2 -> x4, starting transfers between devices: 5.81 us -> 12 us  [ring4(): from_next = lax.ppermute(x, ax, bwd)]
    ppermute x2 -> x4, waiting for transfers between devices: 53.9 us -> 49.5 us  [ring4(): from_next = lax.ppermute(x, ax, bwd)]
  transfers between devices with their start and end apart: 17 -> 24, of which waited for: 11 -> 9; matrix products, arithmetic and copies ran while one was open for 10% -> 18% of each run, Pallas kernels for 19% -> 20%
where the time goes in v5:
time: 264 us; the launch traced here: 262 us
  waiting for transfers between devices  106 us (40%)
  Pallas kernels  52.5 us (20%)
  local copies, waits for them, and re-layouts  37.3 us (14%)
  starting transfers between devices  35.3 us (13%)
  other arithmetic  16.9 us (6%)
  between operations  13.7 us (5%)
    ppermute x4, waiting for transfers between devices, ring4(): from_next = lax.ppermute(x, ax, bwd)  49.5 us
    ppermute x2, waiting for transfers between devices, step(): remote = lax.ppermute(partial, 'xh', SWAP)  35.7 us
    pallas_call x2, Pallas kernels, first_call(): pl.pallas_call(first_kernel, grid_spec=grid, out_shape=[jax.ShapeDtypeStr...  30 us
    pallas_call x2, Pallas kernels, second_call(): pl.pallas_call(lambda s0, h, l, o: second_kernel(h, l, o), grid_spec=grid...  22.5 us
    dynamic_update_slice x12, local copies, waits for them, and re-layouts, ring4(): buf = lax.dynamic_update_slice(buf, jnp.expand_dims(rel[k], at), start)  14 us
    ppermute x4, starting transfers between devices, ring4(): second = lax.ppermute(from_next[h:], ax, bwd)  12.3 us
    ppermute x4, starting transfers between devices, ring4(): from_next = lax.ppermute(x, ax, bwd)  12 us
    ppermute x1, waiting for transfers between devices, step(): pair = lax.ppermute(jnp.stack([left, right]), 'xl', SWAP)  11.2 us
  transfers between devices with their start and end apart: 24, of which 9 were waited for; matrix products, arithmetic and copies ran while one was open for 18% of the time, Pallas kernels for 20%

profile of v5, /device:TPU:1, one launch (start us, length us, event | category | flops | bytes accessed | tf_op | source)
XLA Modules:
  0.0 262.1 jit_solution(2060531785654874933)
XLA Ops:
  7.6 2.1 collective-permute-start
  9.7 11.2 %collective-permute-done = bf16[2,16,16,512]{3,2,1,0:T(8,128)(2,1)S(1)} collective-permute-done((bf16[2,16,16,512]{3,2,1,0:T(8,128)(2,1)S(1)}, bf16[2,16,16,512]{3,2,1,0:T(8,128)(2,1)S(1)}, u32[]{:S(2)}, u32[]{:S(2)}) %collective-permute-start) | collective-permute-done | bytes 524320 | tf_op jit(solution)/shard_map/ppermute | solution.py:116
  22.9 3.2 %collective-permute-start.1 = (bf16[3,16,16,256]{3,2,1,0:T(8,128)(2,1)S(1)}, bf16[3,16,16,256]{3,2,1,0:T(8,128)(2,1)S(1)}, u32[]{:S(2)}, u32[]{:S(2)}) collective-permute-start(bf16[3,16,16,256]{3,2,1,0:T(8,128)(2,1)S(1)} %get-tuple-element.16), channel_id=1, source_target_pairs={{0,3},{1,0},{2,1},{3,2},{4,7},{5,4},{6,5},{7,6},{8,11},{9,8},{10,9... | collective-permute-start | bytes 1179656 | tf_op jit(solution)/shard_map/ppermute | solution.py:18
  26.1 3.8 %collective-permute-start.9 = (bf16[3,16,16,256]{3,2,1,0:T(8,128)(2,1)S(1)}, bf16[3,16,16,256]{3,2,1,0:T(8,128)(2,1)S(1)}, u32[]{:S(2)}, u32[]{:S(2)}) collective-permute-start(bf16[3,16,16,256]{3,2,1,0:T(8,128)(2,1)S(1)} %get-tuple-element.15), channel_id=1, source_target_pairs={{0,12},{4,0},{8,4},{12,8},{1,13},{5,1},{9,5},{13,9},{2,14},{6,2},{... | collective-permute-start | bytes 1179656 | tf_op jit(solution)/shard_map/ppermute | solution.py:18
  30.3 2.7 %collective-permute-done.1 = bf16[3,16,16,256]{3,2,1,0:T(8,128)(2,1)S(1)} collective-permute-done((bf16[3,16,16,256]{3,2,1,0:T(8,128)(2,1)S(1)}, bf16[3,16,16,256]{3,2,1,0:T(8,128)(2,1)S(1)}, u32[]{:S(2)}, u32[]{:S(2)}) %collective-permute-start.1) | collective-permute-done | bytes 393248 | tf_op jit(solution)/shard_map/ppermute | solution.py:18
  33.1 3.5 %collective-permute-start.4 = (bf16[2,16,16,256]{3,2,1,0:T(8,128)(2,1)S(1)}, bf16[2,16,16,256]{3,2,1,0:T(8,128)(2,1)S(1)}, u32[]{:S(2)}, u32[]{:S(2)}) collective-permute-start(bf16[2,16,16,256]{3,2,1,0:T(8,128)(2,1)S(1)} %slice.108), channel_id=1, source_target_pairs={{0,3},{1,0},{2,1},{3,2},{4,7},{5,4},{6,5},{7,6},{8,11},{9,8},{10,9... | collective-permute-start | bytes 786440 | tf_op jit(solution)/shard_map/ppermute | solution.py:21
  36.7 3.8 %collective-permute-start.12 = (bf16[2,16,16,256]{3,2,1,0:T(8,128)(2,1)S(1)}, bf16[2,16,16,256]{3,2,1,0:T(8,128)(2,1)S(1)}, u32[]{:S(2)}, u32[]{:S(2)}) collective-permute-start(bf16[2,16,16,256]{3,2,1,0:T(8,128)(2,1)S(1)} %slice.113), channel_id=1, source_target_pairs={{0,12},{4,0},{8,4},{12,8},{1,13},{5,1},{9,5},{13,9},{2,14},{6,2},{... | collective-permute-start | bytes 786440 | tf_op jit(solution)/shard_map/ppermute | solution.py:21
  40.8 2.8 %collective-permute-done.3 = bf16[1,16,16,256]{3,2,1,0:T(8,128)(2,1)S(1)} collective-permute-done((bf16[1,16,16,256]{3,2,1,0:T(8,128)(2,1)S(1)}, bf16[1,16,16,256]{3,2,1,0:T(8,128)(2,1)S(1)}, u32[]{:S(2)}, u32[]{:S(2)}) %collective-permute-start.3) | collective-permute-done | bytes 131104 | tf_op jit(solution)/shard_map/ppermute | solution.py:20
  43.7 2.6 collective-permute-start.5
  47.2 2.4 collective-permute-start.13
  52.0 46.8 %collective-permute-done.5 = bf16[3,16,4,16,256]{4,3,2,1,0:T(8,128)(2,1)} collective-permute-done((bf16[3,16,4,16,256]{4,3,2,1,0:T(8,128)(2,1)S(1)}, bf16[3,16,4,16,256]{4,3,2,1,0:T(8,128)(2,1)}, u32[]{:S(2)}, u32[]{:S(2)}) %collective-permute-start.5) | collective-permute-done | bytes 1572896 | tf_op jit(solution)/shard_map/ppermute | solution.py:18
  100.1 3.1 %collective-permute-start.8 = (bf16[2,16,4,16,256]{4,3,2,1,0:T(8,128)(2,1)S(1)}, bf16[2,16,4,16,256]{4,3,2,1,0:T(8,128)(2,1)S(1)}, u32[]{:S(2)}, u32[]{:S(2)}) collective-permute-start(bf16[2,16,4,16,256]{4,3,2,1,0:T(8,128)(2,1)S(1)} %slice.110), channel_id=1, source_target_pairs={{0,12},{4,0},{8,4},{12,8},{1,13},{5,1},{9,5},{13,9},{2,14},{6,2},{... | collective-permute-start | bytes 3145736 | tf_op jit(solution)/shard_map/ppermute | solution.py:21
  103.2 3.4 %broadcast.21.clone = bf16[3,16,4,4,16,256]{5,4,3,2,1,0:T(8,128)(2,1)} broadcast(bf16[]{:T(256)} %constant.86.clone.1), dimensions={} | broadcast | bytes 6291458 | tf_op jit(solution)/shard_map/broadcast.2
  111.2 3.4 %broadcast.21.clone.1 = bf16[3,16,4,4,16,256]{5,4,3,2,1,0:T(8,128)(2,1)} broadcast(bf16[]{:T(256)} %constant.86.clone.1), dimensions={} | broadcast | bytes 6291458 | tf_op jit(solution)/shard_map/broadcast.2
  118.3 2.7 %bitcast_dynamic-update-slice_fusion.3 = bf16[3,16,4,4,16,256]{5,4,3,2,1,0:T(8,128)(2,1)} fusion(bf16[3,16,4,4,16,256]{5,4,3,2,1,0:T(8,128)(2,1)} %bitcast_dynamic-update-slice_fusion.4, s32[]{:T(128)S(6)} %select_n.139, bf16[3,16,4,16,256]{4,3,2,1,0:T(8,128)(2,1)} %collective-permute-done.5), kind=kLoop, calls=%fused_computation.12 | loop fusion | bytes 3145732 | tf_op jit(solution)/shard_map/dynamic_update_slice | solution.py:29
  121.0 2.8 %bitcast_dynamic-update-slice_fusion = bf16[3,16,4,4,16,256]{5,4,3,2,1,0:T(8,128)(2,1)} fusion(bf16[3,16,4,4,16,256]{5,4,3,2,1,0:T(8,128)(2,1)} %bitcast_dynamic-update-slice_fusion.1, s32[]{:T(128)S(6)} %select_n.131, bf16[3,16,4,16,256]{4,3,2,1,0:T(8,128)(2,1)} %collective-permute-done.13), kind=kLoop, calls=%fused_computation.9 | loop fusion | bytes 3145732 | tf_op jit(solution)/shard_map/dynamic_update_slice | solution.py:29
  123.8 4.5 %collective-permute-done.7 = bf16[1,16,4,16,256]{4,3,2,1,0:T(8,128)(2,1)S(1)} collective-permute-done((bf16[1,16,4,16,256]{4,3,2,1,0:T(8,128)(2,1)S(1)}, bf16[1,16,4,16,256]{4,3,2,1,0:T(8,128)(2,1)S(1)}, u32[]{:S(2)}, u32[]{:S(2)}) %collective-permute-start.7) | collective-permute-done | bytes 524320 | tf_op jit(solution)/shard_map/ppermute | solution.py:20
  132.9 2.7 %bitcast_dynamic-update-slice_fusion.2.ra.la = bf16[3,16,4,4,16,256]{5,4,3,2,1,0:T(8,128)(2,1)} fusion(bf16[3,16,4,4,16,256]{5,4,3,2,1,0:T(8,128)(2,1)} %fusion, s32[]{:T(128)S(6)} %select_n.143, bf16[3,16,4,16,256]{4,3,2,1,0:T(8,128)(2,1)} %collective-permute-done.6), kind=kLoop, calls=%fused_computation.11 | loop fusion | bytes 3145732 | tf_op jit(solution)/shard_map/dynamic_update_slice | solution.py:29
  135.6 2.8 %bitcast_dynamic-update-slice_fusion.5.rb.lb = bf16[3,16,4,4,16,256]{5,4,3,2,1,0:T(8,128)(2,1)} fusion(bf16[3,16,4,4,16,256]{5,4,3,2,1,0:T(8,128)(2,1)} %fusion.1, s32[]{:T(128)S(6)} %select_n.135, bf16[3,16,4,16,256]{4,3,2,1,0:T(8,128)(2,1)} %collective-permute-done.14), kind=kLoop, calls=%fused_computation.14 | loop fusion | bytes 3145732 | tf_op jit(solution)/shard_map/dynamic_update_slice | solution.py:29
  138.4 15.1 %shard_map.57 = (bf16[12,512,512]{2,1,0:T(8,128)(2,1)}, bf16[12,256,512]{2,1,0:T(8,128)(2,1)}) custom-call(s32[12]{0:T(128)} %get-tuple-element.26.src, s32[12]{0:T(128)} %get-tuple-element.24.s0, s32[12]{0:T(128)} %get-tuple-element.23.s1, s32[1]{0:T(128)} %bitcast.3.xl, bf16[24,512,512]{2,1,0:T(8,128)(2,1)} %psi.3, ...), custom_call_target="tpu_custom_call" | custom-call | flops 4831838208 | bytes 25165824 | tf_op jit(solution)/shard_map/pallas_call | solution.py:76
  153.5 2.7 %constant_dynamic-slice_fusion = bf16[12,128,512]{2,1,0:T(8,128)(2,1)} fusion(bf16[12,256,512]{2,1,0:T(8,128)(2,1)} %get-tuple-element.12, s32[]{:T(128)S(6)} %select_n.147), kind=kLoop, calls=%fused_computation.31 | loop fusion | bytes 3145732 | tf_op jit(solution)/shard_map/dynamic_slice | solution.py:141
  156.1 3.3 %collective-permute-start.21 = (bf16[12,128,512]{2,1,0:T(8,128)(2,1)}, bf16[12,128,512]{2,1,0:T(8,128)(2,1)}, u32[]{:S(2)}, u32[]{:S(2)}) collective-permute-start(bf16[12,128,512]{2,1,0:T(8,128)(2,1)} %constant_dynamic-slice_fusion), channel_id=1, source_target_pairs={{0,32},{32,0},{1,33},{33,1},{2,34},{34,2},{3,35},{35,3},{4,36},{36... | collective-permute-start | bytes 4718600 | tf_op jit(solution)/shard_map/ppermute | solution.py:142
  159.4 14.9 %shard_map.55 = (bf16[12,512,512]{2,1,0:T(8,128)(2,1)}, bf16[12,256,512]{2,1,0:T(8,128)(2,1)}) custom-call(s32[12]{0:T(128)} %get-tuple-element.25.src, s32[12]{0:T(128)} %get-tuple-element.22.s0, s32[12]{0:T(128)} %get-tuple-element.21.s1, s32[1]{0:T(128)} %bitcast.3.xl, bf16[24,512,512]{2,1,0:T(8,128)(2,1)} %psi.3, ...), custom_call_target="tpu_custom_call" | custom-call | flops 4831838208 | bytes 25165824 | tf_op jit(solution)/shard_map/pallas_call | solution.py:76
  174.4 2.8 %constant_dynamic-slice_fusion.2 = bf16[12,128,512]{2,1,0:T(8,128)(2,1)} fusion(bf16[12,256,512]{2,1,0:T(8,128)(2,1)} %get-tuple-element.10, s32[]{:T(128)S(6)} %select_n.147), kind=kLoop, calls=%fused_computation.33 | loop fusion | bytes 3145732 | tf_op jit(solution)/shard_map/dynamic_slice | solution.py:141
  177.2 3.0 %add_convert_fusion.1 = bf16[12,128,512]{2,1,0:T(8,128)(2,1)} fusion(bf16[12,128,512]{2,1,0:T(8,128)(2,1)} %collective-permute-done.21, bf16[12,256,512]{2,1,0:T(8,128)(2,1)S(1)} %copy-done.3, s32[]{:T(128)S(6)} %select_n.146), kind=kLoop, calls=%fused_computation.2 | loop fusion | flops 3145728 | bytes 4718596 | tf_op jit(solution)/shard_map/convert_element_type | solution.py:143
  180.2 2.8 %collective-permute-start.22 = (bf16[12,128,512]{2,1,0:T(8,128)(2,1)}, bf16[12,128,512]{2,1,0:T(8,128)(2,1)S(1)}, u32[]{:S(2)}, u32[]{:S(2)}) collective-permute-start(bf16[12,128,512]{2,1,0:T(8,128)(2,1)} %add_convert_fusion.1), channel_id=1, source_target_pairs={{0,64},{64,0},{1,65},{65,1},{2,66},{66,2},{3,67},{67,3},{4,68},{68... | collective-permute-start | bytes 4718600 | tf_op jit(solution)/shard_map/ppermute | solution.py:144
  183.0 11.3 %shard_map.58 = bf16[12,256,512]{2,1,0:T(8,128)(2,1)} custom-call(s32[12]{0:T(128)} %get-tuple-element.24.s0, bf16[12,512,512]{2,1,0:T(8,128)(2,1)} %get-tuple-element.11.h, bf16[16,256,512]{2,1,0:T(8,128)(2,1)} %bitcast.84), custom_call_target="tpu_custom_call" | custom-call | flops 1610612736 | bytes 12582912 | tf_op jit(solution)/shard_map/pallas_call | solution.py:100
  194.3 2.8 %constant_dynamic-slice_fusion.1 = bf16[12,128,512]{2,1,0:T(8,128)(2,1)} fusion(bf16[12,256,512]{2,1,0:T(8,128)(2,1)} %shard_map.58, s32[]{:T(128)S(6)} %select_n.147), kind=kLoop, calls=%fused_computation.32 | loop fusion | bytes 3145732 | tf_op jit(solution)/shard_map/dynamic_slice | solution.py:149
  200.0 11.3 %shard_map.56 = bf16[12,256,512]{2,1,0:T(8,128)(2,1)} custom-call(s32[12]{0:T(128)} %get-tuple-element.22.s0, bf16[12,512,512]{2,1,0:T(8,128)(2,1)} %get-tuple-element.9.h, bf16[16,256,512]{2,1,0:T(8,128)(2,1)} %bitcast.85), custom_call_target="tpu_custom_call" | custom-call | flops 1610612736 | bytes 12582912 | tf_op jit(solution)/shard_map/pallas_call | solution.py:100
  213.3 4.0 %collective-permute-done.22 = bf16[12,128,512]{2,1,0:T(8,128)(2,1)S(1)} collective-permute-done((bf16[12,128,512]{2,1,0:T(8,128)(2,1)}, bf16[12,128,512]{2,1,0:T(8,128)(2,1)S(1)}, u32[]{:S(2)}, u32[]{:S(2)}) %collective-permute-start.22) | collective-permute-done | bytes 1572896 | tf_op jit(solution)/shard_map/ppermute | solution.py:144
  219.5 31.7 %collective-permute-done.19 = bf16[12,128,512]{2,1,0:T(8,128)(2,1)} collective-permute-done((bf16[12,128,512]{2,1,0:T(8,128)(2,1)S(1)}, bf16[12,128,512]{2,1,0:T(8,128)(2,1)}, u32[]{:S(2)}, u32[]{:S(2)}) %collective-permute-start.19) | collective-permute-done | bytes 1572896 | tf_op jit(solution)/shard_map/ppermute | solution.py:144
  251.2 2.1 add_convert_fusion.2
  (77 shorter events, 30.3 us)
Async XLA Ops:
  6.5 176.5 %all-gather.3.cloned.1.call-start = ((), (), s32[]{:S(2)}) async-start(), calls=%async_computation | async-start | bytes 4456448 | tf_op jit(solution)/shard_map/all_gather | solution.py:127
  7.6 13.3 %collective-permute-start = (bf16[2,16,16,512]{3,2,1,0:T(8,128)(2,1)S(1)}, bf16[2,16,16,512]{3,2,1,0:T(8,128)(2,1)S(1)}, u32[]{:S(2)}, u32[]{:S(2)}) collective-permute-start(bf16[2,16,16,512]{3,2,1,0:T(8,128)(2,1)S(1)} %pad_maximum_fusion.2), channel_id=1, source_target_pairs={{0,16},{16,0},{1,17},{17,1},{2,18},{18,2},{3,19},{19,3},{4,20},{20... | collective-permute-start | bytes 1572872 | tf_op jit(solution)/shard_map/ppermute | solution.py:116
  22.9 10.1 %collective-permute-start.1 = (bf16[3,16,16,256]{3,2,1,0:T(8,128)(2,1)S(1)}, bf16[3,16,16,256]{3,2,1,0:T(8,128)(2,1)S(1)}, u32[]{:S(2)}, u32[]{:S(2)}) collective-permute-start(bf16[3,16,16,256]{3,2,1,0:T(8,128)(2,1)S(1)} %get-tuple-element.16), channel_id=1, source_target_pairs={{0,3},{1,0},{2,1},{3,2},{4,7},{5,4},{6,5},{7,6},{8,11},{9,8},{10,9... | collective-permute-start | bytes 1179656 | tf_op jit(solution)/shard_map/ppermute | solution.py:18
  26.1 10.4 %collective-permute-start.2 = (bf16[3,16,16,256]{3,2,1,0:T(8,128)(2,1)S(1)}, bf16[3,16,16,256]{3,2,1,0:T(8,128)(2,1)S(1)}, u32[]{:S(2)}, u32[]{:S(2)}) collective-permute-start(bf16[3,16,16,256]{3,2,1,0:T(8,128)(2,1)S(1)} %get-tuple-element.16), channel_id=1, source_target_pairs={{0,1},{1,2},{2,3},{3,0},{4,5},{5,6},{6,7},{7,4},{8,9},{9,10},{10,1... | collective-permute-start | bytes 1179656 | tf_op jit(solution)/shard_map/ppermute | solution.py:17
  26.1 10.5 %collective-permute-start.9 = (bf16[3,16,16,256]{3,2,1,0:T(8,128)(2,1)S(1)}, bf16[3,16,16,256]{3,2,1,0:T(8,128)(2,1)S(1)}, u32[]{:S(2)}, u32[]{:S(2)}) collective-permute-start(bf16[3,16,16,256]{3,2,1,0:T(8,128)(2,1)S(1)} %get-tuple-element.15), channel_id=1, source_target_pairs={{0,12},{4,0},{8,4},{12,8},{1,13},{5,1},{9,5},{13,9},{2,14},{6,2},{... | collective-permute-start | bytes 1179656 | tf_op jit(solution)/shard_map/ppermute | solution.py:18
  29.9 10.6 %collective-permute-start.10 = (bf16[3,16,16,256]{3,2,1,0:T(8,128)(2,1)S(1)}, bf16[3,16,16,256]{3,2,1,0:T(8,128)(2,1)S(1)}, u32[]{:S(2)}, u32[]{:S(2)}) collective-permute-start(bf16[3,16,16,256]{3,2,1,0:T(8,128)(2,1)S(1)} %get-tuple-element.15), channel_id=1, source_target_pairs={{0,4},{4,8},{8,12},{12,0},{1,5},{5,9},{9,13},{13,1},{2,6},{6,10},{... | collective-permute-start | bytes 1179656 | tf_op jit(solution)/shard_map/ppermute | solution.py:17
  33.1 10.5 %collective-permute-start.4 = (bf16[2,16,16,256]{3,2,1,0:T(8,128)(2,1)S(1)}, bf16[2,16,16,256]{3,2,1,0:T(8,128)(2,1)S(1)}, u32[]{:S(2)}, u32[]{:S(2)}) collective-permute-start(bf16[2,16,16,256]{3,2,1,0:T(8,128)(2,1)S(1)} %slice.108), channel_id=1, source_target_pairs={{0,3},{1,0},{2,1},{3,2},{4,7},{5,4},{6,5},{7,6},{8,11},{9,8},{10,9... | collective-permute-start | bytes 786440 | tf_op jit(solution)/shard_map/ppermute | solution.py:21
  36.6 7.0 %collective-permute-start.3 = (bf16[1,16,16,256]{3,2,1,0:T(8,128)(2,1)S(1)}, bf16[1,16,16,256]{3,2,1,0:T(8,128)(2,1)S(1)}, u32[]{:S(2)}, u32[]{:S(2)}) collective-permute-start(bf16[1,16,16,256]{3,2,1,0:T(8,128)(2,1)S(1)} %slice.107), channel_id=1, source_target_pairs={{0,1},{1,2},{2,3},{3,0},{4,5},{5,6},{6,7},{7,4},{8,9},{9,10},{10,1... | collective-permute-start | bytes 393224 | tf_op jit(solution)/shard_map/ppermute | solution.py:20
  36.7 10.4 %collective-permute-start.12 = (bf16[2,16,16,256]{3,2,1,0:T(8,128)(2,1)S(1)}, bf16[2,16,16,256]{3,2,1,0:T(8,128)(2,1)S(1)}, u32[]{:S(2)}, u32[]{:S(2)}) collective-permute-start(bf16[2,16,16,256]{3,2,1,0:T(8,128)(2,1)S(1)} %slice.113), channel_id=1, source_target_pairs={{0,12},{4,0},{8,4},{12,8},{1,13},{5,1},{9,5},{13,9},{2,14},{6,2},{... | collective-permute-start | bytes 786440 | tf_op jit(solution)/shard_map/ppermute | solution.py:21
  40.5 6.5 %collective-permute-start.11 = (bf16[1,16,16,256]{3,2,1,0:T(8,128)(2,1)S(1)}, bf16[1,16,16,256]{3,2,1,0:T(8,128)(2,1)S(1)}, u32[]{:S(2)}, u32[]{:S(2)}) collective-permute-start(bf16[1,16,16,256]{3,2,1,0:T(8,128)(2,1)S(1)} %slice.112), channel_id=1, source_target_pairs={{0,4},{4,8},{8,12},{12,0},{1,5},{5,9},{9,13},{13,1},{2,6},{6,10},{... | collective-permute-start | bytes 393224 | tf_op jit(solution)/shard_map/ppermute | solution.py:20
  40.7 9.9 %copy-start.5 = (s32[1,24]{1,0:T(1,128)S(1)}, s32[1,24]{1,0:T(1,128)}, u32[]{:S(2)}) copy-start(s32[1,24]{1,0:T(1,128)} %param.7) | copy-start | bytes 292
  40.7 10.6 %copy-start.4 = (s32[24,2]{0,1:T(2,128)S(1)}, s32[24,2]{0,1:T(2,128)}, u32[]{:S(2)}) copy-start(s32[24,2]{0,1:T(2,128)} %param.6) | copy-start | bytes 580
  43.7 55.1 %collective-permute-start.5 = (bf16[3,16,4,16,256]{4,3,2,1,0:T(8,128)(2,1)S(1)}, bf16[3,16,4,16,256]{4,3,2,1,0:T(8,128)(2,1)}, u32[]{:S(2)}, u32[]{:S(2)}) collective-permute-start(bf16[3,16,4,16,256]{4,3,2,1,0:T(8,128)(2,1)S(1)} %bitcast_dynamic-update-slice_fusion.9), channel_id=1, source_target_pairs={{0,12},{4,0},{8,4},{12,8},{1,13},{5,1},{9,5},{13,9},{2,14},{6,2},{... | collective-permute-start | bytes 4718600 | tf_op jit(solution)/shard_map/ppermute | solution.py:18
  47.2 60.7 %collective-permute-start.13 = (bf16[3,16,4,16,256]{4,3,2,1,0:T(8,128)(2,1)S(1)}, bf16[3,16,4,16,256]{4,3,2,1,0:T(8,128)(2,1)}, u32[]{:S(2)}, u32[]{:S(2)}) collective-permute-start(bf16[3,16,4,16,256]{4,3,2,1,0:T(8,128)(2,1)S(1)} %bitcast_dynamic-update-slice_fusion.6), channel_id=1, source_target_pairs={{0,3},{1,0},{2,1},{3,2},{4,7},{5,4},{6,5},{7,6},{8,11},{9,8},{10,9... | collective-permute-start | bytes 4718600 | tf_op jit(solution)/shard_map/ppermute | solution.py:18
  49.6 66.3 %collective-permute-start.6 = (bf16[3,16,4,16,256]{4,3,2,1,0:T(8,128)(2,1)S(1)}, bf16[3,16,4,16,256]{4,3,2,1,0:T(8,128)(2,1)}, u32[]{:S(2)}, u32[]{:S(2)}) collective-permute-start(bf16[3,16,4,16,256]{4,3,2,1,0:T(8,128)(2,1)S(1)} %bitcast_dynamic-update-slice_fusion.9), channel_id=1, source_target_pairs={{0,4},{4,8},{8,12},{12,0},{1,5},{5,9},{9,13},{13,1},{2,6},{6,10},{... | collective-permute-start | bytes 4718600 | tf_op jit(solution)/shard_map/ppermute | solution.py:17
  50.6 66.5 %collective-permute-start.14 = (bf16[3,16,4,16,256]{4,3,2,1,0:T(8,128)(2,1)S(1)}, bf16[3,16,4,16,256]{4,3,2,1,0:T(8,128)(2,1)}, u32[]{:S(2)}, u32[]{:S(2)}) collective-permute-start(bf16[3,16,4,16,256]{4,3,2,1,0:T(8,128)(2,1)S(1)} %bitcast_dynamic-update-slice_fusion.6), channel_id=1, source_target_pairs={{0,1},{1,2},{2,3},{3,0},{4,5},{5,6},{6,7},{7,4},{8,9},{9,10},{10,1... | collective-permute-start | bytes 4718600 | tf_op jit(solution)/shard_map/ppermute | solution.py:17
  100.1 28.2 %collective-permute-start.8 = (bf16[2,16,4,16,256]{4,3,2,1,0:T(8,128)(2,1)S(1)}, bf16[2,16,4,16,256]{4,3,2,1,0:T(8,128)(2,1)S(1)}, u32[]{:S(2)}, u32[]{:S(2)}) collective-permute-start(bf16[2,16,4,16,256]{4,3,2,1,0:T(8,128)(2,1)S(1)} %slice.110), channel_id=1, source_target_pairs={{0,12},{4,0},{8,4},{12,8},{1,13},{5,1},{9,5},{13,9},{2,14},{6,2},{... | collective-permute-start | bytes 3145736 | tf_op jit(solution)/shard_map/ppermute | solution.py:21
  109.2 22.3 %collective-permute-start.16 = (bf16[2,16,4,16,256]{4,3,2,1,0:T(8,128)(2,1)S(1)}, bf16[2,16,4,16,256]{4,3,2,1,0:T(8,128)(2,1)S(1)}, u32[]{:S(2)}, u32[]{:S(2)}) collective-permute-start(bf16[2,16,4,16,256]{4,3,2,1,0:T(8,128)(2,1)S(1)} %slice.115), channel_id=1, source_target_pairs={{0,3},{1,0},{2,1},{3,2},{4,7},{5,4},{6,5},{7,6},{8,11},{9,8},{10,9... | collective-permute-start | bytes 3145736 | tf_op jit(solution)/shard_map/ppermute | solution.py:21
  117.0 11.3 %collective-permute-start.7 = (bf16[1,16,4,16,256]{4,3,2,1,0:T(8,128)(2,1)S(1)}, bf16[1,16,4,16,256]{4,3,2,1,0:T(8,128)(2,1)S(1)}, u32[]{:S(2)}, u32[]{:S(2)}) collective-permute-start(bf16[1,16,4,16,256]{4,3,2,1,0:T(8,128)(2,1)S(1)} %slice.109), channel_id=1, source_target_pairs={{0,4},{4,8},{8,12},{12,0},{1,5},{5,9},{9,13},{13,1},{2,6},{6,10},{... | collective-permute-start | bytes 1572872 | tf_op jit(solution)/shard_map/ppermute | solution.py:20
  118.2 11.5 %collective-permute-start.15 = (bf16[1,16,4,16,256]{4,3,2,1,0:T(8,128)(2,1)S(1)}, bf16[1,16,4,16,256]{4,3,2,1,0:T(8,128)(2,1)S(1)}, u32[]{:S(2)}, u32[]{:S(2)}) collective-permute-start(bf16[1,16,4,16,256]{4,3,2,1,0:T(8,128)(2,1)S(1)} %slice.114), channel_id=1, source_target_pairs={{0,1},{1,2},{2,3},{3,0},{4,5},{5,6},{6,7},{7,4},{8,9},{9,10},{10,1... | collective-permute-start | bytes 1572872 | tf_op jit(solution)/shard_map/ppermute | solution.py:20
  156.1 21.0 %collective-permute-start.21 = (bf16[12,128,512]{2,1,0:T(8,128)(2,1)}, bf16[12,128,512]{2,1,0:T(8,128)(2,1)}, u32[]{:S(2)}, u32[]{:S(2)}) collective-permute-start(bf16[12,128,512]{2,1,0:T(8,128)(2,1)} %constant_dynamic-slice_fusion), channel_id=1, source_target_pairs={{0,32},{32,0},{1,33},{33,1},{2,34},{34,2},{3,35},{35,3},{4,36},{36... | collective-permute-start | bytes 4718600 | tf_op jit(solution)/shard_map/ppermute | solution.py:142
  174.4 2.8 %copy-start.3 = (bf16[12,256,512]{2,1,0:T(8,128)(2,1)S(1)}, bf16[12,256,512]{2,1,0:T(8,128)(2,1)}, u32[]{:S(2)}) copy-start(bf16[12,256,512]{2,1,0:T(8,128)(2,1)} %get-tuple-element.12) | copy-start | bytes 9437188
  177.2 20.7 %collective-permute-start.18 = (bf16[12,128,512]{2,1,0:T(8,128)(2,1)}, bf16[12,128,512]{2,1,0:T(8,128)(2,1)}, u32[]{:S(2)}, u32[]{:S(2)}) collective-permute-start(bf16[12,128,512]{2,1,0:T(8,128)(2,1)} %constant_dynamic-slice_fusion.2), channel_id=1, source_target_pairs={{0,32},{32,0},{1,33},{33,1},{2,34},{34,2},{3,35},{35,3},{4,36},{36... | collective-permute-start | bytes 4718600 | tf_op jit(solution)/shard_map/ppermute | solution.py:142
  180.2 37.2 %collective-permute-start.22 = (bf16[12,128,512]{2,1,0:T(8,128)(2,1)}, bf16[12,128,512]{2,1,0:T(8,128)(2,1)S(1)}, u32[]{:S(2)}, u32[]{:S(2)}) collective-permute-start(bf16[12,128,512]{2,1,0:T(8,128)(2,1)} %add_convert_fusion.1), channel_id=1, source_target_pairs={{0,64},{64,0},{1,65},{65,1},{2,66},{66,2},{3,67},{67,3},{4,68},{68... | collective-permute-start | bytes 4718600 | tf_op jit(solution)/shard_map/ppermute | solution.py:144
  194.3 3.6 %copy-start.2 = (bf16[12,256,512]{2,1,0:T(8,128)(2,1)S(1)}, bf16[12,256,512]{2,1,0:T(8,128)(2,1)}, u32[]{:S(2)}) copy-start(bf16[12,256,512]{2,1,0:T(8,128)(2,1)} %get-tuple-element.10) | copy-start | bytes 9437188
  197.1 20.3 %collective-permute-start.20 = (bf16[12,128,512]{2,1,0:T(8,128)(2,1)}, bf16[12,128,512]{2,1,0:T(8,128)(2,1)}, u32[]{:S(2)}, u32[]{:S(2)}) collective-permute-start(bf16[12,128,512]{2,1,0:T(8,128)(2,1)} %constant_dynamic-slice_fusion.1), channel_id=1, source_target_pairs={{0,32},{32,0},{1,33},{33,1},{2,34},{34,2},{3,35},{35,3},{4,36},{36... | collective-permute-start | bytes 4718600 | tf_op jit(solution)/shard_map/ppermute | solution.py:150
  199.8 51.4 %collective-permute-start.19 = (bf16[12,128,512]{2,1,0:T(8,128)(2,1)S(1)}, bf16[12,128,512]{2,1,0:T(8,128)(2,1)}, u32[]{:S(2)}, u32[]{:S(2)}) collective-permute-start(bf16[12,128,512]{2,1,0:T(8,128)(2,1)S(1)} %add_convert_fusion.3), channel_id=1, source_target_pairs={{0,64},{64,0},{1,65},{65,1},{2,66},{66,2},{3,67},{67,3},{4,68},{68... | collective-permute-start | bytes 4718600 | tf_op jit(solution)/shard_map/ppermute | solution.py:144
  211.3 6.1 %copy-start = (bf16[12,256,512]{2,1,0:T(8,128)(2,1)S(1)}, bf16[12,256,512]{2,1,0:T(8,128)(2,1)}, u32[]{:S(2)}) copy-start(bf16[12,256,512]{2,1,0:T(8,128)(2,1)} %shard_map.58) | copy-start | bytes 9437188
  213.0 38.2 %copy-start.1 = (bf16[12,256,512]{2,1,0:T(8,128)(2,1)S(1)}, bf16[12,256,512]{2,1,0:T(8,128)(2,1)}, u32[]{:S(2)}) copy-start(bf16[12,256,512]{2,1,0:T(8,128)(2,1)} %shard_map.56) | copy-start | bytes 9437188
  213.0 38.2 %collective-permute-start.17 = (bf16[12,128,512]{2,1,0:T(8,128)(2,1)S(1)}, bf16[12,128,512]{2,1,0:T(8,128)(2,1)S(1)}, u32[]{:S(2)}, u32[]{:S(2)}) collective-permute-start(bf16[12,128,512]{2,1,0:T(8,128)(2,1)S(1)} %constant_dynamic-slice_fusion.3), channel_id=1, source_target_pairs={{0,32},{32,0},{1,33},{33,1},{2,34},{34,2},{3,35},{35,3},{4,36},{36... | collective-permute-start | bytes 4718600 | tf_op jit(solution)/shard_map/ppermute | solution.py:150
Sparse Core Ops, SparseCore 0:
  22.9 73.7 all-gather.2
